TPU v7x, 256 devices: a whole 4x4x8 slice. The times are simulated.
256 devices in a mesh: layer: 64 (over y, z, core), blk: 4 (over x).
Axes of the slice: x: 4, y: 4, z: 8, core: 2. Of those that a mesh axis runs over, the one named last changes fastest.
Arguments:
- mode_matrix: bfloat16 [128, 512, 512], P(None, 'layer', 'blk'), may hold values from -1 to 1, as said below
- decay_rate: bfloat16 [128, 512], P(None, 'layer'), may hold values from 0.0009994507 to 0.29882812
- facet_refl: bfloat16 [128, 512], P(None, 'layer'), may hold values from -0.796875 to 0.796875
Outputs:
- prefix: bfloat16 [64, 4, 512, 512], P('layer', None, 'blk')
Inputs may be any that keep to these rules, and one draw needn't show every extreme that they name: `mode_matrix`: each layer's matrix has orthonormal columns up to the rounding to bfloat16.
All inputs are finite; a program needn't handle non-finite values.
Results may differ from a plain program's by a relative error of at most 0.0045.
The roundings to bfloat16 on the way count: a program that leaves them out, or rounds other values in their place, can miss the bound.
Values may be sent and summed in bfloat16 or wider, within the bound.
No kernel may reach another device: no remote copies, remote signals or barrier semaphores. Data moves between devices by JAX's collectives and lax.ppermute only.
A program may use at most 64 MiB of HBM per device.

v0:
```python
import jax
import jax.numpy as jnp
from jax import lax
from jax.sharding import PartitionSpec as P

HARM = 512
REFL = 4


def passed_along(value, axis, steps):
    count = lax.axis_size(axis)
    first, last = (max(0, -steps), min(count, count - steps))
    return lax.ppermute(value, axis, [(source, source + steps) for source in range(first, last)])


def times_f32(left_op, right_op):
    return jnp.dot(left_op, right_op, preferred_element_type=jnp.float32)


def star_rows(upper_near, upper_far, lower_near, lower_rows):
    coupling_down = times_f32(lower_near[0], upper_far[1]).astype(jnp.bfloat16)
    coupling_up = times_f32(upper_far[1], lower_near[0]).astype(jnp.bfloat16)
    left_sum = upper_near[1]
    for repeat in range(REFL):
        left_sum = (upper_near[1] + times_f32(left_sum, coupling_down)).astype(jnp.bfloat16)
    right_sum = lower_rows[0]
    for repeat in range(REFL):
        right_sum = (lower_rows[0] + times_f32(right_sum, coupling_up)).astype(jnp.bfloat16)
    left_mid = times_f32(left_sum, lower_near[0]).astype(jnp.bfloat16)
    right_mid = times_f32(right_sum, upper_far[1]).astype(jnp.bfloat16)
    new_refl = (upper_near[0] + times_f32(left_mid, upper_far[0])).astype(jnp.bfloat16)
    new_back = times_f32(left_sum, lower_near[1]).astype(jnp.bfloat16)
    new_fore = times_f32(right_sum, upper_far[0]).astype(jnp.bfloat16)
    new_under = (lower_rows[1] + times_f32(right_mid, lower_near[1])).astype(jnp.bfloat16)
    return jnp.stack([new_refl, new_back, new_fore, new_under])


def on_device(mode_matrix, decay_rate, facet_refl):
    relayed_modes, relayed_decay, relayed_refl = (
        lax.all_to_all(mode_matrix, "layer", split_axis=0, concat_axis=1, tiled=True),
        lax.all_to_all(decay_rate, "layer", split_axis=0, concat_axis=1, tiled=True),
        lax.all_to_all(facet_refl, "layer", split_axis=0, concat_axis=1, tiled=True),
    )
    block_index = lax.axis_index("blk")
    row_count = HARM // lax.axis_size("blk")
    row_start = block_index * row_count
    refl_full = relayed_refl.astype(jnp.float32)
    transmit = jnp.sqrt(1.0 - refl_full * refl_full) * jnp.exp(-relayed_decay.astype(jnp.float32))
    mode_piece = lax.all_gather(relayed_modes, "blk", axis=2, tiled=True)
    piece_wide = mode_piece.astype(jnp.float32)
    scaled_refl = (piece_wide * refl_full[:, None, :]).astype(jnp.bfloat16)
    scaled_tran = (piece_wide * transmit[:, None, :]).astype(jnp.bfloat16)
    own_rows = lax.dynamic_slice_in_dim(mode_piece, row_start, row_count, 1)
    refl_part = jnp.einsum(
        "lhm,lkm->lhk", own_rows, scaled_refl, preferred_element_type=jnp.float32
    )
    tran_part = jnp.einsum(
        "lhm,lkm->lhk", own_rows, scaled_tran, preferred_element_type=jnp.float32
    )
    refl_rows = refl_part.astype(jnp.bfloat16)
    tran_rows = tran_part.astype(jnp.bfloat16)
    layer_rows = jnp.stack([refl_rows, tran_rows, tran_rows, -refl_rows], axis=1)
    layer_pair = lax.all_gather(
        jnp.stack([refl_rows, tran_rows], axis=1), "blk", axis=2, tiled=True
    )
    rows_now = layer_rows[0]
    full_now = jnp.stack([layer_pair[0, 0], layer_pair[0, 1], layer_pair[0, 1], -layer_pair[0, 0]])
    rows_now = star_rows(rows_now[0:2], full_now[2:4], layer_pair[1], layer_rows[1, 2:4])
    full_now = lax.all_gather(rows_now, "blk", axis=1, tiled=True)
    group_index = lax.axis_index("layer")
    level_count = lax.axis_size("layer").bit_length() - 1
    for section_level in range(level_count):
        distance = 1 << section_level
        upper_whole = passed_along(full_now, "layer", distance)
        upper_near = lax.dynamic_slice_in_dim(upper_whole[0:2], row_start, row_count, 1)
        upper_far = upper_whole[2:4]
        combined = star_rows(upper_near, upper_far, full_now[0:2], rows_now[2:4])
        rows_now = jnp.where(group_index >= distance, combined, rows_now)
        if section_level + 1 < level_count:
            full_now = lax.all_gather(rows_now, "blk", axis=1, tiled=True)
    return rows_now[None]


def solution(mesh):
    placed = (P(None, "layer", "blk"), P(None, "layer"), P(None, "layer"))
    return jax.shard_map(
        on_device,
        mesh=mesh,
        in_specs=placed,
        out_specs=P("layer", None, "blk", None),
        check_vma=False,
    )
```

profile of v0, /device:TPU:16, one launch (start us, length us, event | category | flops | bytes accessed | tf_op | source)
XLA Modules:
  0.0 783.8 jit_solution(11975169473791905162)
XLA Ops:
  6.5 23.6 %all_to_all.44 = bf16[128,8,128]{2,1,0:T(8,128)(2,1)S(1)} all-to-all(bf16[128,8,128]{2,1,0:T(8,128)(2,1)} %param.3), channel_id=1, replica_groups=mesh['layer'=64,'blk'=4] {'layer'}, dimensions={0} | all-to-all | bytes 524288 | tf_op jit(solution)/shard_map/all_to_all | solution.py:40
  30.9 1.4 copy.19
  32.3 6.5 all-to-all-start.1
  38.8 1.4 copy.21
  40.2 6.3 all-to-all-done.1
  46.5 6.4 all-to-all-start.2
  53.1 7.5 all-to-all-done.2
  60.9 1.8 convolution_convert_fusion.15
  62.7 1.8 convolution_convert_fusion.14
  65.5 30.2 %all-gather.11.cloned.1.call-done = bf16[2,2,512,512]{3,2,0,1:T(8,128)(2,1)} async-done(((bf16[2,2,128,512]{3,2,0,1:T(8,128)(2,1)}), bf16[2,2,512,512]{3,2,0,1:T(8,128)(2,1)}) %all-gather.11.cloned.1.call-update) | async-done | bytes 2097168 | tf_op jit(solution)/shard_map/all_gather | solution.py:63
  95.7 1.8 convolution_convert_fusion.12
  101.8 33.5 %all-gather.13.cloned.1.call-done = bf16[4,512,512]{2,1,0:T(8,128)(2,1)} async-done(((bf16[4,128,512]{2,1,0:T(8,128)(2,1)}), bf16[4,512,512]{2,1,0:T(8,128)(2,1)}) %all-gather.13.cloned.1.call-update) | async-done | bytes 2097168 | tf_op jit(solution)/shard_map/all_gather | solution.py:69
  135.3 1.9 collective-permute-start
  137.3 27.7 %collective-permute-done = bf16[4,512,512]{2,1,0:T(8,128)(2,1)S(1)} collective-permute-done((bf16[4,512,512]{2,1,0:T(8,128)(2,1)}, bf16[4,512,512]{2,1,0:T(8,128)(2,1)S(1)}, u32[]{:S(2)}, u32[]{:S(2)}) %collective-permute-start) | collective-permute-done | bytes 2097184 | tf_op jit(solution)/shard_map/ppermute | solution.py:13
  165.0 1.8 convolution_convert_fusion.10
  167.7 1.5 convolution_convert_fusion.11
  171.3 1.6 fusion.12
  174.2 1.6 fusion.117
  178.0 32.6 %all-gather.15.cloned.1.call-done = bf16[4,512,512]{2,1,0:T(8,128)(2,1)} async-done(((bf16[4,128,512]{2,1,0:T(8,128)(2,1)}), bf16[4,512,512]{2,1,0:T(8,128)(2,1)}) %all-gather.15.cloned.1.call-update) | async-done | bytes 2097168 | tf_op jit(solution)/shard_map/all_gather | solution.py:80
  210.7 3.5 collective-permute-start.1
  214.1 48.2 %collective-permute-done.1 = bf16[4,512,512]{2,1,0:T(8,128)(2,1)} collective-permute-done((bf16[4,512,512]{2,1,0:T(8,128)(2,1)}, bf16[4,512,512]{2,1,0:T(8,128)(2,1)}, u32[]{:S(2)}, u32[]{:S(2)}) %collective-permute-start.1) | collective-permute-done | bytes 2097184 | tf_op jit(solution)/shard_map/ppermute | solution.py:13
  262.4 1.6 convolution_convert_fusion.8
  264.8 1.6 convolution_convert_fusion.9
  268.6 1.6 fusion.17
  271.5 1.6 fusion.116
  275.4 32.6 %all-gather.17.cloned.1.call-done = bf16[4,512,512]{2,1,0:T(8,128)(2,1)} async-done(((bf16[4,128,512]{2,1,0:T(8,128)(2,1)}), bf16[4,512,512]{2,1,0:T(8,128)(2,1)}) %all-gather.17.cloned.1.call-update) | async-done | bytes 2097168 | tf_op jit(solution)/shard_map/all_gather | solution.py:80
  308.1 4.6 collective-permute-start.2
  312.7 93.8 %collective-permute-done.2 = bf16[4,512,512]{2,1,0:T(8,128)(2,1)} collective-permute-done((bf16[4,512,512]{2,1,0:T(8,128)(2,1)}, bf16[4,512,512]{2,1,0:T(8,128)(2,1)}, u32[]{:S(2)}, u32[]{:S(2)}) %collective-permute-start.2) | collective-permute-done | bytes 2097184 | tf_op jit(solution)/shard_map/ppermute | solution.py:13
  406.5 1.6 convolution_convert_fusion.6
  408.9 1.6 convolution_convert_fusion.7
  413.4 1.7 fusion.22
  416.3 1.6 fusion.115
  421.0 32.6 %all-gather.19.cloned.1.call-done = bf16[4,512,512]{2,1,0:T(8,128)(2,1)} async-done(((bf16[4,128,512]{2,1,0:T(8,128)(2,1)}), bf16[4,512,512]{2,1,0:T(8,128)(2,1)}) %all-gather.19.cloned.1.call-update) | async-done | bytes 2097168 | tf_op jit(solution)/shard_map/all_gather | solution.py:80
  453.6 7.6 collective-permute-start.3
  461.3 80.8 %collective-permute-done.3 = bf16[4,512,512]{2,1,0:T(8,128)(2,1)} collective-permute-done((bf16[4,512,512]{2,1,0:T(8,128)(2,1)}, bf16[4,512,512]{2,1,0:T(8,128)(2,1)}, u32[]{:S(2)}, u32[]{:S(2)}) %collective-permute-start.3) | collective-permute-done | bytes 2097184 | tf_op jit(solution)/shard_map/ppermute | solution.py:13
  542.1 1.6 convolution_convert_fusion.4
  545.2 1.6 convolution_convert_fusion.5
  546.8 1.3 slice.446
  549.2 2.0 fusion.55
  551.2 1.7 fusion.27
  552.9 1.4 convolution_convert_fusion.25
  554.3 1.7 fusion.114
  556.0 1.4 convolution_convert_fusion.26
  559.2 44.1 %all-gather.21.cloned.1.call-done = bf16[4,512,512]{2,1,0:T(8,128)(2,1)} async-done(((bf16[4,128,512]{2,1,0:T(8,128)(2,1)}), bf16[4,512,512]{2,1,0:T(8,128)(2,1)}) %all-gather.21.cloned.1.call-update) | async-done | bytes 2097168 | tf_op jit(solution)/shard_map/all_gather | solution.py:80
  603.4 3.1 collective-permute-start.4
  606.5 46.5 %collective-permute-done.4 = bf16[4,512,512]{2,1,0:T(8,128)(2,1)} collective-permute-done((bf16[4,512,512]{2,1,0:T(8,128)(2,1)}, bf16[4,512,512]{2,1,0:T(8,128)(2,1)}, u32[]{:S(2)}, u32[]{:S(2)}) %collective-permute-start.4) | collective-permute-done | bytes 2097184 | tf_op jit(solution)/shard_map/ppermute | solution.py:13
  652.9 1.6 convolution_convert_fusion.2
  656.1 1.6 convolution_convert_fusion.3
  660.1 2.0 fusion.59
  662.0 2.4 fusion.32
  664.4 2.0 convolution_convert_fusion.21
  666.4 2.3 fusion.113
  668.7 1.3 convolution_convert_fusion.22
  670.7 2.1 maximum_select_fusion.4
  672.9 33.6 %all-gather.23.cloned.1.call-done = bf16[4,512,512]{2,1,0:T(8,128)(2,1)} async-done(((bf16[4,128,512]{2,1,0:T(8,128)(2,1)}), bf16[4,512,512]{2,1,0:T(8,128)(2,1)}) %all-gather.23.cloned.1.call-update) | async-done | bytes 2097168 | tf_op jit(solution)/shard_map/all_gather | solution.py:80
  707.7 49.8 %collective-permute-done.5 = bf16[4,512,512]{2,1,0:T(8,128)(2,1)} collective-permute-done((bf16[4,512,512]{2,1,0:T(8,128)(2,1)}, bf16[4,512,512]{2,1,0:T(8,128)(2,1)}, u32[]{:S(2)}, u32[]{:S(2)}) %collective-permute-start.5) | collective-permute-done | bytes 2097184 | tf_op jit(solution)/shard_map/ppermute | solution.py:13
  757.5 1.6 convolution_convert_fusion
  760.6 1.6 convolution_convert_fusion.1
  764.6 2.0 fusion.63
  766.6 2.4 fusion.68
  769.0 2.0 fusion.67
  771.0 2.3 fusion.120
  773.3 1.3 fusion.66
  774.7 2.3 maximum_select_fusion.5
  (120 shorter events, 41.2 us)
Async XLA Ops:
  6.5 54.4 %all-gather.9.cloned.1.call-start = ((), (), s32[]{:S(2)}) async-start(), calls=%async_computation.3 | async-start | bytes 1310720 | tf_op jit(solution)/shard_map/all_gather | solution.py:49
  32.3 14.2 %all-to-all-start.1 = ((bf16[64,2,8]{2,1,0:T(2,128)(2,1)}), bf16[64,2,8]{2,1,0:T(2,128)(2,1)S(1)}, u32[]{:S(2)}, u32[]{:S(2)}) async-start(bf16[64,2,8]{2,1,0:T(2,128)(2,1)} %bitcast.3), calls=%async_computation.1 | async-start | bytes 65536 | tf_op jit(solution)/shard_map/all_to_all | solution.py:42
  46.5 14.1 %all-to-all-start.2 = ((bf16[64,2,8]{2,1,0:T(2,128)(2,1)}), bf16[64,2,8]{2,1,0:T(2,128)(2,1)S(1)}, u32[]{:S(2)}, u32[]{:S(2)}) async-start(bf16[64,2,8]{2,1,0:T(2,128)(2,1)} %bitcast.6), calls=%async_computation.2 | async-start | bytes 65536 | tf_op jit(solution)/shard_map/all_to_all | solution.py:41
  52.9 42.8 %all-gather.11.cloned.1.call-start = ((), (), s32[]{:S(2)}) async-start(), calls=%async_computation.4 | async-start | bytes 2621440 | tf_op jit(solution)/shard_map/all_gather | solution.py:63
  65.4 69.9 %all-gather.13.cloned.1.call-start = ((), (), s32[]{:S(2)}) async-start(), calls=%async_computation.5 | async-start | bytes 2621440 | tf_op jit(solution)/shard_map/all_gather | solution.py:69
  95.7 2.6 copy-start.22
  101.7 108.9 %all-gather.15.cloned.1.call-start = ((), (), s32[]{:S(2)}) async-start(), calls=%async_computation.6 | async-start | bytes 2621440 | tf_op jit(solution)/shard_map/all_gather | solution.py:80
  135.3 29.7 %collective-permute-start = (bf16[4,512,512]{2,1,0:T(8,128)(2,1)}, bf16[4,512,512]{2,1,0:T(8,128)(2,1)S(1)}, u32[]{:S(2)}, u32[]{:S(2)}) collective-permute-start(bf16[4,512,512]{2,1,0:T(8,128)(2,1)} %all-gather.13.cloned.1.call-done), channel_id=1, source_target_pairs={{0,4},{4,8},{8,12},{12,16},{16,20},{20,24},{24,28},{28,32},{32,36}... | collective-permute-start | bytes 6291464 | tf_op jit(solution)/shard_map/ppermute | solution.py:13
  165.0 2.7 copy-start.20
  178.0 86.0 %copy-start.1 = (bf16[4,128,512]{2,1,0:T(8,128)(2,1)S(1)}, bf16[4,128,512]{2,1,0:T(8,128)(2,1)}, u32[]{:S(2)}) copy-start(bf16[4,128,512]{2,1,0:T(8,128)(2,1)} %maximum_select_fusion) | copy-start | bytes 1572868
  178.0 130.1 %all-gather.17.cloned.1.call-start = ((), (), s32[]{:S(2)}) async-start(), calls=%async_computation.7 | async-start | bytes 2621440 | tf_op jit(solution)/shard_map/all_gather | solution.py:80
  210.7 51.7 %collective-permute-start.1 = (bf16[4,512,512]{2,1,0:T(8,128)(2,1)}, bf16[4,512,512]{2,1,0:T(8,128)(2,1)}, u32[]{:S(2)}, u32[]{:S(2)}) collective-permute-start(bf16[4,512,512]{2,1,0:T(8,128)(2,1)} %all-gather.15.cloned.1.call-done), channel_id=1, source_target_pairs={{0,8},{4,12},{8,16},{12,20},{16,24},{20,28},{24,32},{28,36},{32,40... | collective-permute-start | bytes 6291464 | tf_op jit(solution)/shard_map/ppermute | solution.py:13
  275.4 132.7 %copy-start.2 = (bf16[4,128,512]{2,1,0:T(8,128)(2,1)S(1)}, bf16[4,128,512]{2,1,0:T(8,128)(2,1)}, u32[]{:S(2)}) copy-start(bf16[4,128,512]{2,1,0:T(8,128)(2,1)} %maximum_select_fusion.1) | copy-start | bytes 1572868
  275.4 178.2 %all-gather.19.cloned.1.call-start = ((), (), s32[]{:S(2)}) async-start(), calls=%async_computation.8 | async-start | bytes 2621440 | tf_op jit(solution)/shard_map/all_gather | solution.py:80
  308.1 98.4 %collective-permute-start.2 = (bf16[4,512,512]{2,1,0:T(8,128)(2,1)}, bf16[4,512,512]{2,1,0:T(8,128)(2,1)}, u32[]{:S(2)}, u32[]{:S(2)}) collective-permute-start(bf16[4,512,512]{2,1,0:T(8,128)(2,1)} %all-gather.17.cloned.1.call-done), channel_id=1, source_target_pairs={{0,16},{4,20},{8,24},{12,28},{16,32},{20,36},{24,40},{28,44},{32,4... | collective-permute-start | bytes 6291464 | tf_op jit(solution)/shard_map/ppermute | solution.py:13
  413.4 2.9 copy-start.21
  419.2 0.7 copy-start.5
  420.9 122.8 %copy-start.3 = (bf16[4,128,512]{2,1,0:T(8,128)(2,1)S(1)}, bf16[4,128,512]{2,1,0:T(8,128)(2,1)}, u32[]{:S(2)}) copy-start(bf16[4,128,512]{2,1,0:T(8,128)(2,1)} %maximum_select_fusion.2) | copy-start | bytes 1572868
  420.9 182.4 %all-gather.21.cloned.1.call-start = ((), (), s32[]{:S(2)}) async-start(), calls=%async_computation.9 | async-start | bytes 2621440 | tf_op jit(solution)/shard_map/all_gather | solution.py:80
  453.6 88.5 %collective-permute-start.3 = (bf16[4,512,512]{2,1,0:T(8,128)(2,1)}, bf16[4,512,512]{2,1,0:T(8,128)(2,1)}, u32[]{:S(2)}, u32[]{:S(2)}) collective-permute-start(bf16[4,512,512]{2,1,0:T(8,128)(2,1)} %all-gather.19.cloned.1.call-done), channel_id=1, source_target_pairs={{0,32},{4,36},{8,40},{12,44},{16,48},{20,52},{24,56},{28,60},{32,6... | collective-permute-start | bytes 6291464 | tf_op jit(solution)/shard_map/ppermute | solution.py:13
  551.2 6.9 copy-start.6
  552.9 6.3 copy-start.9
  554.3 4.9 copy-start.12
  556.0 3.2 copy-start.15
  557.4 0.7 copy-start.18
  559.1 95.4 %copy-start.4 = (bf16[4,128,512]{2,1,0:T(8,128)(2,1)S(1)}, bf16[4,128,512]{2,1,0:T(8,128)(2,1)}, u32[]{:S(2)}) copy-start(bf16[4,128,512]{2,1,0:T(8,128)(2,1)} %maximum_select_fusion.3) | copy-start | bytes 1572868
  559.2 147.3 %all-gather.23.cloned.1.call-start = ((), (), s32[]{:S(2)}) async-start(), calls=%async_computation.10 | async-start | bytes 2621440 | tf_op jit(solution)/shard_map/all_gather | solution.py:80
  603.4 49.6 %collective-permute-start.4 = (bf16[4,512,512]{2,1,0:T(8,128)(2,1)}, bf16[4,512,512]{2,1,0:T(8,128)(2,1)}, u32[]{:S(2)}, u32[]{:S(2)}) collective-permute-start(bf16[4,512,512]{2,1,0:T(8,128)(2,1)} %all-gather.21.cloned.1.call-done), channel_id=1, source_target_pairs={{0,64},{4,68},{8,72},{12,76},{16,80},{20,84},{24,88},{28,92},{32,9... | collective-permute-start | bytes 6291464 | tf_op jit(solution)/shard_map/ppermute | solution.py:13
  662.0 8.7 %copy-start.7 = (bf16[128,512]{1,0:T(8,128)(2,1)S(1)}, bf16[128,512]{1,0:T(8,128)(2,1)}, u32[]{:S(2)}) copy-start(bf16[128,512]{1,0:T(8,128)(2,1)} %copy-done.5) | copy-start | bytes 393220
  662.0 8.7 %copy-start.10 = (bf16[128,512]{1,0:T(8,128)(2,1)S(1)}, bf16[128,512]{1,0:T(8,128)(2,1)}, u32[]{:S(2)}) copy-start(bf16[128,512]{1,0:T(8,128)(2,1)} %copy-done.9) | copy-start | bytes 393220
  662.0 8.7 %copy-start.13 = (bf16[128,512]{1,0:T(8,128)(2,1)S(1)}, bf16[128,512]{1,0:T(8,128)(2,1)}, u32[]{:S(2)}) copy-start(bf16[128,512]{1,0:T(8,128)(2,1)} %copy-done.12) | copy-start | bytes 393220
  662.0 8.7 %copy-start.16 = (bf16[128,512]{1,0:T(8,128)(2,1)S(1)}, bf16[128,512]{1,0:T(8,128)(2,1)}, u32[]{:S(2)}) copy-start(bf16[128,512]{1,0:T(8,128)(2,1)} %copy-done.15) | copy-start | bytes 393220
  670.1 0.7 copy-start.19
  672.8 86.3 %copy-start = (bf16[4,128,512]{2,1,0:T(8,128)(2,1)S(1)}, bf16[4,128,512]{2,1,0:T(8,128)(2,1)}, u32[]{:S(2)}) copy-start(bf16[4,128,512]{2,1,0:T(8,128)(2,1)} %maximum_select_fusion.4) | copy-start | bytes 1572868
  706.4 51.1 %collective-permute-start.5 = (bf16[4,512,512]{2,1,0:T(8,128)(2,1)}, bf16[4,512,512]{2,1,0:T(8,128)(2,1)}, u32[]{:S(2)}, u32[]{:S(2)}) collective-permute-start(bf16[4,512,512]{2,1,0:T(8,128)(2,1)} %all-gather.23.cloned.1.call-done), channel_id=1, source_target_pairs={{0,128},{4,132},{8,136},{12,140},{16,144},{20,148},{24,152},{28,15... | collective-permute-start | bytes 6291464 | tf_op jit(solution)/shard_map/ppermute | solution.py:13
  766.6 8.0 %copy-start.8 = (bf16[128,512]{1,0:T(8,128)(2,1)S(1)}, bf16[128,512]{1,0:T(8,128)(2,1)}, u32[]{:S(2)}) copy-start(bf16[128,512]{1,0:T(8,128)(2,1)} %copy-done.5) | copy-start | bytes 393220
  766.6 8.1 %copy-start.11 = (bf16[128,512]{1,0:T(8,128)(2,1)S(1)}, bf16[128,512]{1,0:T(8,128)(2,1)}, u32[]{:S(2)}) copy-start(bf16[128,512]{1,0:T(8,128)(2,1)} %copy-done.9) | copy-start | bytes 393220
  766.6 8.1 %copy-start.14 = (bf16[128,512]{1,0:T(8,128)(2,1)S(1)}, bf16[128,512]{1,0:T(8,128)(2,1)}, u32[]{:S(2)}) copy-start(bf16[128,512]{1,0:T(8,128)(2,1)} %copy-done.12) | copy-start | bytes 393220
  766.6 8.1 %copy-start.17 = (bf16[128,512]{1,0:T(8,128)(2,1)S(1)}, bf16[128,512]{1,0:T(8,128)(2,1)}, u32[]{:S(2)}) copy-start(bf16[128,512]{1,0:T(8,128)(2,1)} %copy-done.15) | copy-start | bytes 393220
Sparse Core Ops, SparseCore 0:
  31.0 25.5 all-gather.8
  65.5 30.0 all-gather.10
  101.9 33.4 all-gather.12
  178.1 32.5 all-gather.14
  275.5 32.5 all-gather.16
  421.0 32.5 all-gather.18
  559.3 44.0 all-gather.20
  673.0 33.4 all-gather.22
where the time goes:
time: 786 us; the launch traced here: 784 us
  waiting for transfers between devices  600 us (76%)
  matrix products  86.9 us (11%)
  starting transfers between devices  35.1 us (4%)
  blocking collectives  23.6 us (3%)
  between operations  14.3 us (2%)
  local copies, waits for them, and re-layouts  13.7 us (2%)
  other arithmetic  10.2 us (1%)
    ppermute x6, waiting for transfers between devices, passed_along(): lax.ppermute(value, axis, [(source, source + steps) for source in range(f...  347 us
    all_gather x6, waiting for transfers between devices, on_device(): full_now = lax.all_gather(rows_now, 'blk', axis=1, tiled=True)  209 us
    dot_general x70, matrix products, times_f32(): return jnp.dot(left_op, right_op, preferred_element_type=jnp.float32)  83.3 us
    all_gather x1, waiting for transfers between devices, on_device(): lax.all_gather(jnp.stack([refl_rows, tran_rows], axis=1), 'blk', axis=2,...  30.2 us
    all_to_all x1, blocking collectives, on_device(): lax.all_to_all(mode_matrix, 'layer', split_axis=0, concat_axis=1, tiled=T...  23.6 us
    ppermute x6, starting transfers between devices, passed_along(): lax.ppermute(value, axis, [(source, source + steps) for source in range(f...  22 us
  transfers between devices with their start and end apart: 16, of which 15 were waited for; matrix products, arithmetic and copies ran while one was open for 0% of the time, Pallas kernels for 0%

commit v1 on v0

v1 whole, which is shorter than its diff:
```python
import jax
import jax.numpy as jnp
from jax import lax
from jax.sharding import PartitionSpec as P

HARM = 512
REFL = 4


def passed_along(value, axis, steps):
    count = lax.axis_size(axis)
    first, last = (max(0, -steps), min(count, count - steps))
    return lax.ppermute(value, axis, [(source, source + steps) for source in range(first, last)])


def times_f32(left_op, right_op):
    return jnp.dot(left_op, right_op, preferred_element_type=jnp.float32)


def star_whole(upper_s, lower_s):
    coupling_down = times_f32(lower_s[0], upper_s[3]).astype(jnp.bfloat16)
    coupling_up = times_f32(upper_s[3], lower_s[0]).astype(jnp.bfloat16)
    left_sum = upper_s[1]
    for repeat in range(REFL):
        left_sum = (upper_s[1] + times_f32(left_sum, coupling_down)).astype(jnp.bfloat16)
    right_sum = lower_s[2]
    for repeat in range(REFL):
        right_sum = (lower_s[2] + times_f32(right_sum, coupling_up)).astype(jnp.bfloat16)
    left_mid = times_f32(left_sum, lower_s[0]).astype(jnp.bfloat16)
    right_mid = times_f32(right_sum, upper_s[3]).astype(jnp.bfloat16)
    new_refl = (upper_s[0] + times_f32(left_mid, upper_s[2])).astype(jnp.bfloat16)
    new_back = times_f32(left_sum, lower_s[1]).astype(jnp.bfloat16)
    new_fore = times_f32(right_sum, upper_s[2]).astype(jnp.bfloat16)
    new_under = (lower_s[3] + times_f32(right_mid, lower_s[1])).astype(jnp.bfloat16)
    return jnp.stack([new_refl, new_back, new_fore, new_under])


def on_device(mode_matrix, decay_rate, facet_refl):
    relayed_modes, relayed_decay, relayed_refl = (
        lax.all_to_all(mode_matrix, "layer", split_axis=0, concat_axis=1, tiled=True),
        lax.all_to_all(decay_rate, "layer", split_axis=0, concat_axis=1, tiled=True),
        lax.all_to_all(facet_refl, "layer", split_axis=0, concat_axis=1, tiled=True),
    )
    block_index = lax.axis_index("blk")
    row_count = HARM // lax.axis_size("blk")
    row_start = block_index * row_count
    refl_full = relayed_refl.astype(jnp.float32)
    transmit = jnp.sqrt(1.0 - refl_full * refl_full) * jnp.exp(-relayed_decay.astype(jnp.float32))
    modes_all = lax.all_gather(relayed_modes, "blk", axis=2, tiled=True)
    modes_wide = modes_all.astype(jnp.float32)
    scaled_refl = (modes_wide * refl_full[:, None, :]).astype(jnp.bfloat16)
    scaled_tran = (modes_wide * transmit[:, None, :]).astype(jnp.bfloat16)
    refl_blk = jnp.einsum(
        "lhm,lkm->lhk", modes_all, scaled_refl, preferred_element_type=jnp.float32
    ).astype(jnp.bfloat16)
    tran_blk = jnp.einsum(
        "lhm,lkm->lhk", modes_all, scaled_tran, preferred_element_type=jnp.float32
    ).astype(jnp.bfloat16)
    layer_s = jnp.stack([refl_blk, tran_blk, tran_blk, -refl_blk], axis=1)
    whole_now = layer_s[0]
    for layer_pos in range(1, layer_s.shape[0]):
        whole_now = star_whole(whole_now, layer_s[layer_pos])
    group_index = lax.axis_index("layer")
    level_count = lax.axis_size("layer").bit_length() - 1
    for section_level in range(level_count):
        distance = 1 << section_level
        upper_whole = passed_along(whole_now, "layer", distance)
        combined = star_whole(upper_whole, whole_now)
        whole_now = jnp.where(group_index >= distance, combined, whole_now)
    own_rows = lax.dynamic_slice_in_dim(whole_now, row_start, row_count, 1)
    return own_rows[None]


def solution(mesh):
    placed = (P(None, "layer", "blk"), P(None, "layer"), P(None, "layer"))
    return jax.shard_map(
        on_device,
        mesh=mesh,
        in_specs=placed,
        out_specs=P("layer", None, "blk", None),
        check_vma=False,
    )
```

time: 786 us -> 719 us (0.915)
  the two profiles are of different devices: /device:TPU:16 before, /device:TPU:118 now
where the time goes in v1:
time: 719 us; the launch traced here: 708 us
  waiting for transfers between devices  399 us (55%)
  matrix products  179 us (25%)
  starting transfers between devices  63.1 us (9%)
  other arithmetic  26 us (4%)
  blocking collectives  20.6 us (3%)
  between operations  14.3 us (2%)
    ppermute x6, waiting for transfers between devices, passed_along(): lax.ppermute(value, axis, [(source, source + steps) for source in range(f...  390 us
    dot_general x70, matrix products, times_f32(): return jnp.dot(left_op, right_op, preferred_element_type=jnp.float32)  176 us
    ppermute x6, starting transfers between devices, passed_along(): lax.ppermute(value, axis, [(source, source + steps) for source in range(f...  45.9 us
    select_n x6, other arithmetic, on_device(): whole_now = jnp.where(group_index >= distance, combined, whole_now)  24.4 us
    all_to_all x1, blocking collectives, on_device(): lax.all_to_all(mode_matrix, 'layer', split_axis=0, concat_axis=1, tiled=T...  20.6 us
  transfers between devices with their start and end apart: 9, of which 8 were waited for; matrix products, arithmetic and copies ran while one was open for 0% of the time, Pallas kernels for 0%

profile of v1, /device:TPU:118, one launch (start us, length us, event | category | flops | bytes accessed | tf_op | source)
XLA Modules:
  0.0 708.0 jit_solution(2434654861357009096)
XLA Ops:
  6.5 20.6 %all_to_all.44 = bf16[128,8,128]{2,1,0:T(8,128)(2,1)S(1)} all-to-all(bf16[128,8,128]{2,1,0:T(8,128)(2,1)} %param.3), channel_id=1, replica_groups=mesh['layer'=64,'blk'=4] {'layer'}, dimensions={0} | all-to-all | bytes 524288 | tf_op jit(solution)/shard_map/all_to_all | solution.py:40
  29.3 8.2 %all-to-all-start.1 = ((bf16[64,2,8]{2,1,0:T(2,128)(2,1)}), bf16[64,2,8]{2,1,0:T(2,128)(2,1)S(1)}, u32[]{:S(2)}, u32[]{:S(2)}) async-start(bf16[64,2,8]{2,1,0:T(2,128)(2,1)} %bitcast.3), calls=%async_computation.1 | async-start | bytes 65536 | tf_op jit(solution)/shard_map/all_to_all | solution.py:42
  38.9 3.7 all-to-all-done.1
  42.6 8.9 %all-to-all-start.2 = ((bf16[64,2,8]{2,1,0:T(2,128)(2,1)}), bf16[64,2,8]{2,1,0:T(2,128)(2,1)S(1)}, u32[]{:S(2)}, u32[]{:S(2)}) async-start(bf16[64,2,8]{2,1,0:T(2,128)(2,1)} %bitcast.7), calls=%async_computation.2 | async-start | bytes 65536 | tf_op jit(solution)/shard_map/all_to_all | solution.py:41
  51.7 4.9 all-to-all-done.2
  79.1 25.4 %collective-permute-done = bf16[4,512,512]{1,2,0:T(8,128)(2,1)} collective-permute-done((bf16[4,512,512]{1,2,0:T(8,128)(2,1)}, bf16[4,512,512]{1,2,0:T(8,128)(2,1)}, u32[]{:S(2)}, u32[]{:S(2)}) %collective-permute-start) | collective-permute-done | bytes 2097184 | tf_op jit(solution)/shard_map/ppermute | solution.py:13
  106.1 3.1 fusion.38
  114.2 2.8 fusion.41
  117.1 3.1 fusion.43
  122.3 2.4 fusion.95
  124.8 2.8 fusion.87
  127.6 2.6 maximum_select_fusion
  130.2 4.3 collective-permute-start.1
  134.5 43.7 %collective-permute-done.1 = bf16[4,512,512]{1,2,0:T(8,128)(2,1)} collective-permute-done((bf16[4,512,512]{1,2,0:T(8,128)(2,1)}, bf16[4,512,512]{1,2,0:T(8,128)(2,1)}, u32[]{:S(2)}, u32[]{:S(2)}) %collective-permute-start.1) | collective-permute-done | bytes 2097184 | tf_op jit(solution)/shard_map/ppermute | solution.py:13
  178.3 2.5 convolution_convert_fusion.33
  180.7 3.4 fusion.44
  184.1 3.3 fusion.46
  189.9 2.5 convolution_convert_fusion.31
  192.4 3.3 fusion.47
  195.6 3.3 fusion.49
  199.0 3.2 fusion.115
  202.1 2.4 fusion.97
  204.6 3.2 fusion.86
  207.7 3.2 maximum_select_fusion.1
  210.9 4.3 collective-permute-start.2
  215.2 111.5 %collective-permute-done.2 = bf16[4,512,512]{1,2,0:T(8,128)(2,1)} collective-permute-done((bf16[4,512,512]{1,2,0:T(8,128)(2,1)}, bf16[4,512,512]{1,2,0:T(8,128)(2,1)}, u32[]{:S(2)}, u32[]{:S(2)}) %collective-permute-start.2) | collective-permute-done | bytes 2097184 | tf_op jit(solution)/shard_map/ppermute | solution.py:13
  326.7 2.5 convolution_convert_fusion.29
  329.2 3.3 fusion.50
  332.5 3.3 fusion.52
  335.9 2.4 fusion.98
  338.3 2.5 convolution_convert_fusion.27
  340.8 3.6 fusion.53
  344.4 3.4 fusion.55
  347.8 3.2 fusion.116
  351.0 2.5 fusion.99
  353.5 3.2 fusion.85
  356.7 5.1 maximum_select_fusion.2
  361.8 31.4 %collective-permute-start.3 = (bf16[4,512,512]{1,2,0:T(8,128)(2,1)}, bf16[4,512,512]{1,2,0:T(8,128)(2,1)}, u32[]{:S(2)}, u32[]{:S(2)}) collective-permute-start(bf16[4,512,512]{1,2,0:T(8,128)(2,1)} %maximum_select_fusion.2), channel_id=1, source_target_pairs={{0,32},{4,36},{8,40},{12,44},{16,48},{20,52},{24,56},{28,60},{32,6... | collective-permute-start | bytes 6291464 | tf_op jit(solution)/shard_map/ppermute | solution.py:13
  393.2 114.2 %collective-permute-done.3 = bf16[4,512,512]{1,2,0:T(8,128)(2,1)} collective-permute-done((bf16[4,512,512]{1,2,0:T(8,128)(2,1)}, bf16[4,512,512]{1,2,0:T(8,128)(2,1)}, u32[]{:S(2)}, u32[]{:S(2)}) %collective-permute-start.3) | collective-permute-done | bytes 2097184 | tf_op jit(solution)/shard_map/ppermute | solution.py:13
  507.4 2.5 convolution_convert_fusion.25
  509.9 3.4 fusion.56
  513.3 3.4 fusion.58
  516.7 2.5 fusion.100
  519.1 2.5 convolution_convert_fusion.23
  521.6 3.4 fusion.59
  525.0 3.3 fusion.61
  528.3 3.2 fusion.117
  531.4 2.4 fusion.101
  533.9 3.2 fusion.84
  537.1 5.4 maximum_select_fusion.3
  544.6 47.0 %collective-permute-done.4 = bf16[4,512,512]{1,2,0:T(8,128)(2,1)} collective-permute-done((bf16[4,512,512]{1,2,0:T(8,128)(2,1)}, bf16[4,512,512]{1,2,0:T(8,128)(2,1)}, u32[]{:S(2)}, u32[]{:S(2)}) %collective-permute-start.4) | collective-permute-done | bytes 2097184 | tf_op jit(solution)/shard_map/ppermute | solution.py:13
  591.6 2.5 convolution_convert_fusion.21
  594.1 3.3 fusion.62
  597.4 3.3 fusion.64
  603.1 2.5 convolution_convert_fusion.19
  605.6 3.5 fusion.65
  609.1 3.3 fusion.67
  612.4 3.1 fusion.118
  615.5 2.5 fusion.103
  618.0 3.2 fusion.83
  621.2 6.9 maximum_select_fusion.4
  629.7 48.0 %collective-permute-done.5 = bf16[4,512,512]{1,2,0:T(8,128)(2,1)S(1)} collective-permute-done((bf16[4,512,512]{1,2,0:T(8,128)(2,1)}, bf16[4,512,512]{1,2,0:T(8,128)(2,1)S(1)}, u32[]{:S(2)}, u32[]{:S(2)}) %collective-permute-start.5) | collective-permute-done | bytes 2097184 | tf_op jit(solution)/shard_map/ppermute | solution.py:13
  679.6 3.1 fusion.71
  688.1 2.7 fusion.70
  (63 shorter events, 60.4 us)
Async XLA Ops:
  6.5 50.4 %all-gather.2.cloned.1.call-start = ((), (), s32[]{:S(2)}) async-start(), calls=%async_computation.3 | async-start | bytes 1310720 | tf_op jit(solution)/shard_map/all_gather | solution.py:49
  29.3 13.3 %all-to-all-start.1 = ((bf16[64,2,8]{2,1,0:T(2,128)(2,1)}), bf16[64,2,8]{2,1,0:T(2,128)(2,1)S(1)}, u32[]{:S(2)}, u32[]{:S(2)}) async-start(bf16[64,2,8]{2,1,0:T(2,128)(2,1)} %bitcast.3), calls=%async_computation.1 | async-start | bytes 65536 | tf_op jit(solution)/shard_map/all_to_all | solution.py:42
  42.6 14.0 %all-to-all-start.2 = ((bf16[64,2,8]{2,1,0:T(2,128)(2,1)}), bf16[64,2,8]{2,1,0:T(2,128)(2,1)S(1)}, u32[]{:S(2)}, u32[]{:S(2)}) async-start(bf16[64,2,8]{2,1,0:T(2,128)(2,1)} %bitcast.7), calls=%async_computation.2 | async-start | bytes 65536 | tf_op jit(solution)/shard_map/all_to_all | solution.py:41
  59.3 1.0 copy-start.5
  59.3 1.5 copy-start.6
  59.3 2.0 copy-start.2
  60.2 7.9 %copy-start.7 = (bf16[512,512]{1,0:T(8,128)(2,1)}, bf16[512,512]{1,0:T(8,128)(2,1)S(1)}, u32[]{:S(2)}) copy-start(bf16[512,512]{1,0:T(8,128)(2,1)S(1)} %convolution_convert_fusion.41) | copy-start | bytes 1572868
  71.0 0.8 copy-start.4
  76.9 27.7 %collective-permute-start = (bf16[4,512,512]{1,2,0:T(8,128)(2,1)}, bf16[4,512,512]{1,2,0:T(8,128)(2,1)}, u32[]{:S(2)}, u32[]{:S(2)}) collective-permute-start(bf16[4,512,512]{1,2,0:T(8,128)(2,1)} %pad_maximum_fusion), channel_id=1, source_target_pairs={{0,4},{4,8},{8,12},{12,16},{16,20},{20,24},{24,28},{28,32},{32,36}... | collective-permute-start | bytes 6291464 | tf_op jit(solution)/shard_map/ppermute | solution.py:13
  111.5 5.6 copy-start
  130.2 48.0 %collective-permute-start.1 = (bf16[4,512,512]{1,2,0:T(8,128)(2,1)}, bf16[4,512,512]{1,2,0:T(8,128)(2,1)}, u32[]{:S(2)}, u32[]{:S(2)}) collective-permute-start(bf16[4,512,512]{1,2,0:T(8,128)(2,1)} %maximum_select_fusion), channel_id=1, source_target_pairs={{0,8},{4,12},{8,16},{12,20},{16,24},{20,28},{24,32},{28,36},{32,40... | collective-permute-start | bytes 6291464 | tf_op jit(solution)/shard_map/ppermute | solution.py:13
  210.9 115.8 %collective-permute-start.2 = (bf16[4,512,512]{1,2,0:T(8,128)(2,1)}, bf16[4,512,512]{1,2,0:T(8,128)(2,1)}, u32[]{:S(2)}, u32[]{:S(2)}) collective-permute-start(bf16[4,512,512]{1,2,0:T(8,128)(2,1)} %maximum_select_fusion.1), channel_id=1, source_target_pairs={{0,16},{4,20},{8,24},{12,28},{16,32},{20,36},{24,40},{28,44},{32,4... | collective-permute-start | bytes 6291464 | tf_op jit(solution)/shard_map/ppermute | solution.py:13
  361.8 145.5 %collective-permute-start.3 = (bf16[4,512,512]{1,2,0:T(8,128)(2,1)}, bf16[4,512,512]{1,2,0:T(8,128)(2,1)}, u32[]{:S(2)}, u32[]{:S(2)}) collective-permute-start(bf16[4,512,512]{1,2,0:T(8,128)(2,1)} %maximum_select_fusion.2), channel_id=1, source_target_pairs={{0,32},{4,36},{8,40},{12,44},{16,48},{20,52},{24,56},{28,60},{32,6... | collective-permute-start | bytes 6291464 | tf_op jit(solution)/shard_map/ppermute | solution.py:13
  542.4 49.2 %collective-permute-start.4 = (bf16[4,512,512]{1,2,0:T(8,128)(2,1)}, bf16[4,512,512]{1,2,0:T(8,128)(2,1)}, u32[]{:S(2)}, u32[]{:S(2)}) collective-permute-start(bf16[4,512,512]{1,2,0:T(8,128)(2,1)} %maximum_select_fusion.3), channel_id=1, source_target_pairs={{0,64},{4,68},{8,72},{12,76},{16,80},{20,84},{24,88},{28,92},{32,9... | collective-permute-start | bytes 6291464 | tf_op jit(solution)/shard_map/ppermute | solution.py:13
  628.1 49.6 %collective-permute-start.5 = (bf16[4,512,512]{1,2,0:T(8,128)(2,1)}, bf16[4,512,512]{1,2,0:T(8,128)(2,1)S(1)}, u32[]{:S(2)}, u32[]{:S(2)}) collective-permute-start(bf16[4,512,512]{1,2,0:T(8,128)(2,1)} %maximum_select_fusion.4), channel_id=1, source_target_pairs={{0,128},{4,132},{8,136},{12,140},{16,144},{20,148},{24,152},{28,15... | collective-permute-start | bytes 6291464 | tf_op jit(solution)/shard_map/ppermute | solution.py:13
  677.8 10.4 %copy-start.1 = (bf16[4,512,512]{1,2,0:T(8,128)(2,1)}, bf16[4,512,512]{1,2,0:T(8,128)(2,1)S(1)}, u32[]{:S(2)}) copy-start(bf16[4,512,512]{1,2,0:T(8,128)(2,1)S(1)} %collective-permute-done.5) | copy-start | bytes 6291460
  692.4 3.8 copy-start.3
Sparse Core Ops, SparseCore 0:
  28.0 26.8 all-gather.1

commit v2 on v1

--- a/solution.py
+++ b/solution.py
@@ -2,6 +2,8 @@
 import jax.numpy as jnp
 from jax import lax
 from jax.sharding import PartitionSpec as P
+from jax.experimental import pallas as pl
+from jax.experimental.pallas import tpu as pltpu
 
 HARM = 512
 REFL = 4
@@ -32,7 +34,35 @@
     new_back = times_f32(left_sum, lower_s[1]).astype(jnp.bfloat16)
     new_fore = times_f32(right_sum, upper_s[2]).astype(jnp.bfloat16)
     new_under = (lower_s[3] + times_f32(right_mid, lower_s[1])).astype(jnp.bfloat16)
-    return jnp.stack([new_refl, new_back, new_fore, new_under])
+    return [new_refl, new_back, new_fore, new_under]
+
+
+def star_kernel(flag_ref, upper_ref, lower_ref, out_ref):
+    @pl.when(flag_ref[0] == 0)
+    def _keep():
+        out_ref[...] = lower_ref[...]
+
+    @pl.when(flag_ref[0] != 0)
+    def _combine():
+        upper_s = [upper_ref[i] for i in range(4)]
+        lower_s = [lower_ref[i] for i in range(4)]
+        new_s = star_whole(upper_s, lower_s)
+        for i in range(4):
+            out_ref[i] = new_s[i]
+
+
+def star_call(active, upper_s, lower_s):
+    flag = active.astype(jnp.int32).reshape(1)
+    return pl.pallas_call(
+        star_kernel,
+        out_shape=jax.ShapeDtypeStruct(lower_s.shape, lower_s.dtype),
+        in_specs=[
+            pl.BlockSpec(memory_space=pltpu.SMEM),
+            pl.BlockSpec(memory_space=pltpu.VMEM),
+            pl.BlockSpec(memory_space=pltpu.VMEM),
+        ],
+        out_specs=pl.BlockSpec(memory_space=pltpu.VMEM),
+    )(flag, upper_s, lower_s)
 
 
 def on_device(mode_matrix, decay_rate, facet_refl):
@@ -59,14 +89,13 @@
     layer_s = jnp.stack([refl_blk, tran_blk, tran_blk, -refl_blk], axis=1)
     whole_now = layer_s[0]
     for layer_pos in range(1, layer_s.shape[0]):
-        whole_now = star_whole(whole_now, layer_s[layer_pos])
+        whole_now = star_call(jnp.array(True), whole_now, layer_s[layer_pos])
     group_index = lax.axis_index("layer")
     level_count = lax.axis_size("layer").bit_length() - 1
     for section_level in range(level_count):
         distance = 1 << section_level
         upper_whole = passed_along(whole_now, "layer", distance)
-        combined = star_whole(upper_whole, whole_now)
-        whole_now = jnp.where(group_index >= distance, combined, whole_now)
+        whole_now = star_call(group_index >= distance, upper_whole, whole_now)
     own_rows = lax.dynamic_slice_in_dim(whole_now, row_start, row_count, 1)
     return own_rows[None]
 

time: 719 us -> 595 us (0.83)
  the two profiles are of different devices: /device:TPU:118 before, /device:TPU:116 now
where the time goes in v2:
time: 595 us
  waiting for transfers between devices  445 us (75%)
  Pallas kernels  56.6 us (10%)
  starting transfers between devices  38.9 us (7%)
  blocking collectives  20.6 us (3%)
  local copies, waits for them, and re-layouts  16.2 us (3%)
  between operations  13.6 us (2%)
    ppermute x6, waiting for transfers between devices, passed_along(): lax.ppermute(value, axis, [(source, source + steps) for source in range(f...  437 us
    pallas_call x7, Pallas kernels, star_call(): pl.pallas_call(star_kernel, out_shape=jax.ShapeDtypeStruct(lower_s.shape,...  56.6 us
    ppermute x6, starting transfers between devices, passed_along(): lax.ppermute(value, axis, [(source, source + steps) for source in range(f...  21.7 us
    all_to_all x1, blocking collectives, on_device(): lax.all_to_all(mode_matrix, 'layer', split_axis=0, concat_axis=1, tiled=T...  20.6 us
  transfers between devices with their start and end apart: 9, of which 8 were waited for; matrix products, arithmetic and copies ran while one was open for 1% of the time, Pallas kernels for 0%

profile of v2, /device:TPU:116, one launch (start us, length us, event | category | flops | bytes accessed | tf_op | source)
XLA Modules:
  0.0 594.9 jit_solution(12555619370766418992)
XLA Ops:
  6.5 0.0 all-gather.2.cloned.1.call-start
  6.5 20.6 %all_to_all.44 = bf16[128,8,128]{2,1,0:T(8,128)(2,1)S(1)} all-to-all(bf16[128,8,128]{2,1,0:T(8,128)(2,1)} %param.3), channel_id=1, replica_groups=mesh['layer'=64,'blk'=4] {'layer'}, dimensions={0} | all-to-all | bytes 524288 | tf_op jit(solution)/shard_map/all_to_all | solution.py:70
  27.1 0.7 copy.39
  27.8 0.0 all-gather.2.cloned.1.call-update
  27.9 1.4 copy.28
  29.3 8.2 %all-to-all-start.1 = ((bf16[64,2,8]{2,1,0:T(2,128)(2,1)}), bf16[64,2,8]{2,1,0:T(2,128)(2,1)S(1)}, u32[]{:S(2)}, u32[]{:S(2)}) async-start(bf16[64,2,8]{2,1,0:T(2,128)(2,1)} %bitcast.9), calls=%async_computation.1 | async-start | bytes 65536 | tf_op jit(solution)/shard_map/all_to_all | solution.py:72
  37.5 1.4 copy.31
  38.9 3.7 all-to-all-done.1
  42.6 9.0 %all-to-all-start.2 = ((bf16[64,2,8]{2,1,0:T(2,128)(2,1)}), bf16[64,2,8]{2,1,0:T(2,128)(2,1)S(1)}, u32[]{:S(2)}, u32[]{:S(2)}) async-start(bf16[64,2,8]{2,1,0:T(2,128)(2,1)} %bitcast.14), calls=%async_computation.2 | async-start | bytes 65536 | tf_op jit(solution)/shard_map/all_to_all | solution.py:71
  51.6 0.1 reshape.84
  51.7 5.0 all-to-all-done.2
  56.7 0.1 copy.32
  56.8 0.1 copy.33
  56.9 0.1 exp.15
  57.0 0.0 all-gather.2.cloned.1.call-done
  57.0 0.0 copy-start.6
  57.1 2.4 fusion.6
  59.4 0.1 fusion.15
  59.5 0.0 copy-done.6
  59.5 0.8 fusion.12
  60.3 0.6 pad_maximum_fusion
  60.9 2.3 slice_bitcast_fusion
  63.2 8.1 %shard_map.37.lower_ref = bf16[4,512,512]{2,1,0:T(8,128)(2,1)} custom-call(s32[1]{0:T(128)} %constant.11.clone.1.flag_ref, bf16[4,512,512]{2,1,0:T(8,128)(2,1)} %get-tuple-element.6.upper_ref, bf16[4,512,512]{2,1,0:T(8,128)(2,1)} %get-tuple-element.5.lower_ref), custom_call_target="tpu_custom_call" | custom-call | tf_op jit(solution)/shard_map/pallas_call | solution.py:56
  71.3 1.9 collective-permute-start
  73.2 25.6 %collective-permute-done.upper_ref = bf16[4,512,512]{2,1,0:T(8,128)(2,1)S(1)} collective-permute-done((bf16[4,512,512]{2,1,0:T(8,128)(2,1)}, bf16[4,512,512]{2,1,0:T(8,128)(2,1)S(1)}, u32[]{:S(2)}, u32[]{:S(2)}) %collective-permute-start) | collective-permute-done | bytes 2097184 | tf_op jit(solution)/shard_map/ppermute | solution.py:15
  98.8 0.0 copy-start.1
  98.8 1.4 copy-done.1
  100.2 8.1 %shard_map.38.lower_ref = bf16[4,512,512]{2,1,0:T(8,128)(2,1)} custom-call(s32[1]{0:T(128)} %bitcast.5.flag_ref, bf16[4,512,512]{2,1,0:T(8,128)(2,1)} %copy-done.1, bf16[4,512,512]{2,1,0:T(8,128)(2,1)} %shard_map.37.lower_ref), custom_call_target="tpu_custom_call" | custom-call | tf_op jit(solution)/shard_map/pallas_call | solution.py:56
  108.2 4.1 collective-permute-start.1
  112.3 44.2 %collective-permute-done.1.upper_ref = bf16[4,512,512]{2,1,0:T(8,128)(2,1)S(1)} collective-permute-done((bf16[4,512,512]{2,1,0:T(8,128)(2,1)}, bf16[4,512,512]{2,1,0:T(8,128)(2,1)S(1)}, u32[]{:S(2)}, u32[]{:S(2)}) %collective-permute-start.1) | collective-permute-done | bytes 2097184 | tf_op jit(solution)/shard_map/ppermute | solution.py:15
  156.6 0.0 copy-start.2
  156.6 1.4 copy-done.2
  157.9 8.1 %shard_map.39.lower_ref = bf16[4,512,512]{2,1,0:T(8,128)(2,1)} custom-call(s32[1]{0:T(128)} %bitcast.4.flag_ref, bf16[4,512,512]{2,1,0:T(8,128)(2,1)} %copy-done.2, bf16[4,512,512]{2,1,0:T(8,128)(2,1)} %shard_map.38.lower_ref), custom_call_target="tpu_custom_call" | custom-call | tf_op jit(solution)/shard_map/pallas_call | solution.py:56
  166.0 3.8 collective-permute-start.2
  169.8 89.4 %collective-permute-done.2.upper_ref = bf16[4,512,512]{2,1,0:T(8,128)(2,1)S(1)} collective-permute-done((bf16[4,512,512]{2,1,0:T(8,128)(2,1)}, bf16[4,512,512]{2,1,0:T(8,128)(2,1)S(1)}, u32[]{:S(2)}, u32[]{:S(2)}) %collective-permute-start.2) | collective-permute-done | bytes 2097184 | tf_op jit(solution)/shard_map/ppermute | solution.py:15
  259.2 0.0 copy-start.3
  259.2 1.4 copy-done.3
  260.6 8.1 %shard_map.40.lower_ref = bf16[4,512,512]{2,1,0:T(8,128)(2,1)} custom-call(s32[1]{0:T(128)} %bitcast.3.flag_ref, bf16[4,512,512]{2,1,0:T(8,128)(2,1)} %copy-done.3, bf16[4,512,512]{2,1,0:T(8,128)(2,1)} %shard_map.39.lower_ref), custom_call_target="tpu_custom_call" | custom-call | tf_op jit(solution)/shard_map/pallas_call | solution.py:56
  268.6 8.7 %collective-permute-start.3 = (bf16[4,512,512]{2,1,0:T(8,128)(2,1)}, bf16[4,512,512]{2,1,0:T(8,128)(2,1)S(1)}, u32[]{:S(2)}, u32[]{:S(2)}) collective-permute-start(bf16[4,512,512]{2,1,0:T(8,128)(2,1)} %shard_map.40.lower_ref), channel_id=1, source_target_pairs={{0,32},{4,36},{8,40},{12,44},{16,48},{20,52},{24,56},{28,60},{32,6... | collective-permute-start | bytes 6291464 | tf_op jit(solution)/shard_map/ppermute | solution.py:15
  277.4 181.8 %collective-permute-done.3.upper_ref = bf16[4,512,512]{2,1,0:T(8,128)(2,1)S(1)} collective-permute-done((bf16[4,512,512]{2,1,0:T(8,128)(2,1)}, bf16[4,512,512]{2,1,0:T(8,128)(2,1)S(1)}, u32[]{:S(2)}, u32[]{:S(2)}) %collective-permute-start.3) | collective-permute-done | bytes 2097184 | tf_op jit(solution)/shard_map/ppermute | solution.py:15
  459.2 0.0 copy-start.4
  459.2 1.4 copy-done.4
  460.5 8.1 %shard_map.41.lower_ref = bf16[4,512,512]{2,1,0:T(8,128)(2,1)} custom-call(s32[1]{0:T(128)} %bitcast.2.flag_ref, bf16[4,512,512]{2,1,0:T(8,128)(2,1)} %copy-done.4, bf16[4,512,512]{2,1,0:T(8,128)(2,1)} %shard_map.40.lower_ref), custom_call_target="tpu_custom_call" | custom-call | tf_op jit(solution)/shard_map/pallas_call | solution.py:56
  468.6 1.9 collective-permute-start.4
  470.5 47.1 %collective-permute-done.4.upper_ref = bf16[4,512,512]{2,1,0:T(8,128)(2,1)S(1)} collective-permute-done((bf16[4,512,512]{2,1,0:T(8,128)(2,1)}, bf16[4,512,512]{2,1,0:T(8,128)(2,1)S(1)}, u32[]{:S(2)}, u32[]{:S(2)}) %collective-permute-start.4) | collective-permute-done | bytes 2097184 | tf_op jit(solution)/shard_map/ppermute | solution.py:15
  517.7 0.0 copy-start.5
  517.7 1.4 copy-done.5
  519.0 8.1 %shard_map.42.lower_ref = bf16[4,512,512]{2,1,0:T(8,128)(2,1)} custom-call(s32[1]{0:T(128)} %bitcast.1.flag_ref, bf16[4,512,512]{2,1,0:T(8,128)(2,1)} %copy-done.5, bf16[4,512,512]{2,1,0:T(8,128)(2,1)} %shard_map.41.lower_ref), custom_call_target="tpu_custom_call" | custom-call | tf_op jit(solution)/shard_map/pallas_call | solution.py:56
  527.1 1.3 collective-permute-start.5
  528.4 48.3 %collective-permute-done.5.upper_ref = bf16[4,512,512]{2,1,0:T(8,128)(2,1)S(1)} collective-permute-done((bf16[4,512,512]{2,1,0:T(8,128)(2,1)}, bf16[4,512,512]{2,1,0:T(8,128)(2,1)S(1)}, u32[]{:S(2)}, u32[]{:S(2)}) %collective-permute-start.5) | collective-permute-done | bytes 2097184 | tf_op jit(solution)/shard_map/ppermute | solution.py:15
  576.7 0.0 copy-start
  576.7 1.3 copy-done
  578.1 8.1 %shard_map.43 = bf16[4,512,512]{2,1,0:T(8,128)(2,1)} custom-call(s32[1]{0:T(128)} %bitcast.flag_ref, bf16[4,512,512]{2,1,0:T(8,128)(2,1)} %copy-done, bf16[4,512,512]{2,1,0:T(8,128)(2,1)} %shard_map.42.lower_ref), custom_call_target="tpu_custom_call" | custom-call | tf_op jit(solution)/shard_map/pallas_call | solution.py:56
  586.2 1.9 dynamic-slice_bitcast_fusion
  (4 shorter events, 0.1 us)
Async XLA Ops:
  6.5 50.5 %all-gather.2.cloned.1.call-start = ((), (), s32[]{:S(2)}) async-start(), calls=%async_computation.3 | async-start | bytes 1310720 | tf_op jit(solution)/shard_map/all_gather | solution.py:79
  29.3 13.3 %all-to-all-start.1 = ((bf16[64,2,8]{2,1,0:T(2,128)(2,1)}), bf16[64,2,8]{2,1,0:T(2,128)(2,1)S(1)}, u32[]{:S(2)}, u32[]{:S(2)}) async-start(bf16[64,2,8]{2,1,0:T(2,128)(2,1)} %bitcast.9), calls=%async_computation.1 | async-start | bytes 65536 | tf_op jit(solution)/shard_map/all_to_all | solution.py:72
  42.6 14.1 %all-to-all-start.2 = ((bf16[64,2,8]{2,1,0:T(2,128)(2,1)}), bf16[64,2,8]{2,1,0:T(2,128)(2,1)S(1)}, u32[]{:S(2)}, u32[]{:S(2)}) async-start(bf16[64,2,8]{2,1,0:T(2,128)(2,1)} %bitcast.14), calls=%async_computation.2 | async-start | bytes 65536 | tf_op jit(solution)/shard_map/all_to_all | solution.py:71
  57.0 2.5 copy-start.6
  71.3 27.6 %collective-permute-start = (bf16[4,512,512]{2,1,0:T(8,128)(2,1)}, bf16[4,512,512]{2,1,0:T(8,128)(2,1)S(1)}, u32[]{:S(2)}, u32[]{:S(2)}) collective-permute-start(bf16[4,512,512]{2,1,0:T(8,128)(2,1)} %shard_map.37.lower_ref), channel_id=1, source_target_pairs={{0,4},{4,8},{8,12},{12,16},{16,20},{20,24},{24,28},{28,32},{32,36}... | collective-permute-start | bytes 6291464 | tf_op jit(solution)/shard_map/ppermute | solution.py:15
  98.8 1.4 copy-start.1
  108.2 48.3 %collective-permute-start.1 = (bf16[4,512,512]{2,1,0:T(8,128)(2,1)}, bf16[4,512,512]{2,1,0:T(8,128)(2,1)S(1)}, u32[]{:S(2)}, u32[]{:S(2)}) collective-permute-start(bf16[4,512,512]{2,1,0:T(8,128)(2,1)} %shard_map.38.lower_ref), channel_id=1, source_target_pairs={{0,8},{4,12},{8,16},{12,20},{16,24},{20,28},{24,32},{28,36},{32,40... | collective-permute-start | bytes 6291464 | tf_op jit(solution)/shard_map/ppermute | solution.py:15
  156.6 1.4 copy-start.2
  166.0 93.2 %collective-permute-start.2 = (bf16[4,512,512]{2,1,0:T(8,128)(2,1)}, bf16[4,512,512]{2,1,0:T(8,128)(2,1)S(1)}, u32[]{:S(2)}, u32[]{:S(2)}) collective-permute-start(bf16[4,512,512]{2,1,0:T(8,128)(2,1)} %shard_map.39.lower_ref), channel_id=1, source_target_pairs={{0,16},{4,20},{8,24},{12,28},{16,32},{20,36},{24,40},{28,44},{32,4... | collective-permute-start | bytes 6291464 | tf_op jit(solution)/shard_map/ppermute | solution.py:15
  259.2 1.4 copy-start.3
  268.6 190.5 %collective-permute-start.3 = (bf16[4,512,512]{2,1,0:T(8,128)(2,1)}, bf16[4,512,512]{2,1,0:T(8,128)(2,1)S(1)}, u32[]{:S(2)}, u32[]{:S(2)}) collective-permute-start(bf16[4,512,512]{2,1,0:T(8,128)(2,1)} %shard_map.40.lower_ref), channel_id=1, source_target_pairs={{0,32},{4,36},{8,40},{12,44},{16,48},{20,52},{24,56},{28,60},{32,6... | collective-permute-start | bytes 6291464 | tf_op jit(solution)/shard_map/ppermute | solution.py:15
  459.2 1.4 copy-start.4
  468.6 49.1 %collective-permute-start.4 = (bf16[4,512,512]{2,1,0:T(8,128)(2,1)}, bf16[4,512,512]{2,1,0:T(8,128)(2,1)S(1)}, u32[]{:S(2)}, u32[]{:S(2)}) collective-permute-start(bf16[4,512,512]{2,1,0:T(8,128)(2,1)} %shard_map.41.lower_ref), channel_id=1, source_target_pairs={{0,64},{4,68},{8,72},{12,76},{16,80},{20,84},{24,88},{28,92},{32,9... | collective-permute-start | bytes 6291464 | tf_op jit(solution)/shard_map/ppermute | solution.py:15
  517.7 1.4 copy-start.5
  527.1 49.6 %collective-permute-start.5 = (bf16[4,512,512]{2,1,0:T(8,128)(2,1)}, bf16[4,512,512]{2,1,0:T(8,128)(2,1)S(1)}, u32[]{:S(2)}, u32[]{:S(2)}) collective-permute-start(bf16[4,512,512]{2,1,0:T(8,128)(2,1)} %shard_map.42.lower_ref), channel_id=1, source_target_pairs={{0,128},{4,132},{8,136},{12,140},{16,144},{20,148},{24,152},{28,15... | collective-permute-start | bytes 6291464 | tf_op jit(solution)/shard_map/ppermute | solution.py:15
  576.7 1.3 copy-start
Sparse Core Ops, SparseCore 0:
  28.0 27.1 all-gather.1

commit v3 on v2

--- a/solution.py
+++ b/solution.py
@@ -1,3 +1,5 @@
+import functools
+
 import jax
 import jax.numpy as jnp
 from jax import lax
@@ -13,6 +15,11 @@
     count = lax.axis_size(axis)
     first, last = (max(0, -steps), min(count, count - steps))
     return lax.ppermute(value, axis, [(source, source + steps) for source in range(first, last)])
+
+
+def rotated(value, axis, steps):
+    count = lax.axis_size(axis)
+    return lax.ppermute(value, axis, [(source, (source + steps) % count) for source in range(count)])
 
 
 def times_f32(left_op, right_op):
@@ -37,43 +44,69 @@
     return [new_refl, new_back, new_fore, new_under]
 
 
-def star_kernel(flag_ref, upper_ref, lower_ref, out_ref):
-    @pl.when(flag_ref[0] == 0)
+def star_kernel(ctl_ref, upper_ref, lower_ref, out_ref, rows_ref, *, piece_count):
+    active = ctl_ref[0]
+    own_piece = ctl_ref[1]
+    row_count = rows_ref.shape[1]
+
+    @pl.when(active == 0)
     def _keep():
         out_ref[...] = lower_ref[...]
 
-    @pl.when(flag_ref[0] != 0)
+    @pl.when(active != 0)
     def _combine():
-        upper_s = [upper_ref[i] for i in range(4)]
-        lower_s = [lower_ref[i] for i in range(4)]
+        if piece_count:
+            upper_s = [
+                jnp.concatenate(
+                    [
+                        upper_ref[(own_piece - source + piece_count) % piece_count, block]
+                        for source in range(piece_count)
+                    ],
+                    axis=0,
+                )
+                for block in range(4)
+            ]
+        else:
+            upper_s = [upper_ref[block] for block in range(4)]
+        lower_s = [lower_ref[block] for block in range(4)]
         new_s = star_whole(upper_s, lower_s)
-        for i in range(4):
-            out_ref[i] = new_s[i]
+        for block in range(4):
+            out_ref[block] = new_s[block]
+
+    row_start = pl.multiple_of(own_piece * row_count, row_count)
+    for block in range(4):
+        rows_ref[block] = out_ref[block, pl.ds(row_start, row_count), :]
 
 
-def star_call(active, upper_s, lower_s):
-    flag = active.astype(jnp.int32).reshape(1)
+def star_call(active, own_piece, piece_count, upper_s, lower_s):
+    ctl = jnp.stack([active.astype(jnp.int32), own_piece.astype(jnp.int32)])
+    row_count = lower_s.shape[1] // max(piece_count, 1) if piece_count else lower_s.shape[1] // 4
     return pl.pallas_call(
-        star_kernel,
-        out_shape=jax.ShapeDtypeStruct(lower_s.shape, lower_s.dtype),
+        functools.partial(star_kernel, piece_count=piece_count),
+        out_shape=(
+            jax.ShapeDtypeStruct(lower_s.shape, lower_s.dtype),
+            jax.ShapeDtypeStruct((4, row_count, lower_s.shape[2]), lower_s.dtype),
+        ),
         in_specs=[
             pl.BlockSpec(memory_space=pltpu.SMEM),
             pl.BlockSpec(memory_space=pltpu.VMEM),
             pl.BlockSpec(memory_space=pltpu.VMEM),
         ],
-        out_specs=pl.BlockSpec(memory_space=pltpu.VMEM),
-    )(flag, upper_s, lower_s)
+        out_specs=(
+            pl.BlockSpec(memory_space=pltpu.VMEM),
+            pl.BlockSpec(memory_space=pltpu.VMEM),
+        ),
+    )(ctl, upper_s, lower_s)
 
 
 def on_device(mode_matrix, decay_rate, facet_refl):
-    relayed_modes, relayed_decay, relayed_refl = (
-        lax.all_to_all(mode_matrix, "layer", split_axis=0, concat_axis=1, tiled=True),
-        lax.all_to_all(decay_rate, "layer", split_axis=0, concat_axis=1, tiled=True),
-        lax.all_to_all(facet_refl, "layer", split_axis=0, concat_axis=1, tiled=True),
-    )
+    coefficients = jnp.stack([decay_rate, facet_refl], axis=-1)
+    relayed_modes = lax.all_to_all(mode_matrix, "layer", split_axis=0, concat_axis=1, tiled=True)
+    relayed_coeff = lax.all_to_all(coefficients, "layer", split_axis=0, concat_axis=1, tiled=True)
+    relayed_decay = relayed_coeff[..., 0]
+    relayed_refl = relayed_coeff[..., 1]
     block_index = lax.axis_index("blk")
-    row_count = HARM // lax.axis_size("blk")
-    row_start = block_index * row_count
+    block_count = lax.axis_size("blk")
     refl_full = relayed_refl.astype(jnp.float32)
     transmit = jnp.sqrt(1.0 - refl_full * refl_full) * jnp.exp(-relayed_decay.astype(jnp.float32))
     modes_all = lax.all_gather(relayed_modes, "blk", axis=2, tiled=True)
@@ -88,15 +121,22 @@
     ).astype(jnp.bfloat16)
     layer_s = jnp.stack([refl_blk, tran_blk, tran_blk, -refl_blk], axis=1)
     whole_now = layer_s[0]
+    own_rows = None
     for layer_pos in range(1, layer_s.shape[0]):
-        whole_now = star_call(jnp.array(True), whole_now, layer_s[layer_pos])
+        whole_now, own_rows = star_call(
+            jnp.array(True), block_index, 0, whole_now, layer_s[layer_pos]
+        )
     group_index = lax.axis_index("layer")
     level_count = lax.axis_size("layer").bit_length() - 1
     for section_level in range(level_count):
         distance = 1 << section_level
-        upper_whole = passed_along(whole_now, "layer", distance)
-        whole_now = star_call(group_index >= distance, upper_whole, whole_now)
-    own_rows = lax.dynamic_slice_in_dim(whole_now, row_start, row_count, 1)
+        upper_rows = passed_along(own_rows, "layer", distance)
+        pieces = [upper_rows] + [
+            rotated(upper_rows, "blk", shift) for shift in range(1, block_count)
+        ]
+        whole_now, own_rows = star_call(
+            group_index >= distance, block_index, block_count, jnp.stack(pieces), whole_now
+        )
     return own_rows[None]
 
 

time: 595 us -> 425 us (0.71)
  the two profiles are of different devices: /device:TPU:116 before, /device:TPU:16 now
where the time goes in v3:
time: 425 us; the launch traced here: 417 us
  waiting for transfers between devices  244 us (57%)
  Pallas kernels  58.4 us (14%)
  starting transfers between devices  54.7 us (13%)
  blocking collectives  23.6 us (6%)
  other arithmetic  15.4 us (4%)
  between operations  14 us (3%)
    ppermute x18, waiting for transfers between devices, rotated(): lax.ppermute(value, axis, [(source, (source + steps) % count) for source...  127 us
    ppermute x6, waiting for transfers between devices, passed_along(): lax.ppermute(value, axis, [(source, source + steps) for source in range(f...  100 us
    pallas_call x7, Pallas kernels, star_call(): pl.pallas_call(functools.partial(star_kernel, piece_count=piece_count), o...  58.4 us
    ppermute x18, starting transfers between devices, rotated(): lax.ppermute(value, axis, [(source, (source + steps) % count) for source...  30.1 us
    all_to_all x1, blocking collectives, on_device(): lax.all_to_all(mode_matrix, 'layer', split_axis=0, concat_axis=1, tiled=T...  23.6 us
    ppermute x6, starting transfers between devices, passed_along(): lax.ppermute(value, axis, [(source, source + steps) for source in range(f...  18.1 us
    another operation x6, other arithmetic, on_device(): jnp.stack(pieces)  9.74 us
    all_gather x1, waiting for transfers between devices, on_device(): modes_all = lax.all_gather(relayed_modes, 'blk', axis=2, tiled=True)  9.56 us
  transfers between devices with their start and end apart: 26, of which 21 were waited for; matrix products, arithmetic and copies ran while one was open for 1% of the time, Pallas kernels for 0%

profile of v3, /device:TPU:16, one launch (start us, length us, event | category | flops | bytes accessed | tf_op | source)
XLA Modules:
  0.0 417.4 jit_solution(3312854847798747348)
XLA Ops:
  6.5 23.6 %all_to_all.36 = bf16[128,8,128]{2,1,0:T(8,128)(2,1)S(1)} all-to-all(bf16[128,8,128]{2,1,0:T(8,128)(2,1)} %param.3), channel_id=1, replica_groups=mesh['layer'=64,'blk'=4] {'layer'}, dimensions={0} | all-to-all | bytes 524288 | tf_op jit(solution)/shard_map/all_to_all | solution.py:104
  30.2 0.7 copy.44
  30.9 0.7 pad_maximum_fusion.7
  31.6 0.7 copy.26
  32.4 6.5 %all-to-all-start.1 = ((bf16[128,8,2]{1,2,0:T(2,128)(2,1)}), bf16[128,8,2]{1,2,0:T(2,128)(2,1)S(1)}, u32[]{:S(2)}, u32[]{:S(2)}) async-start(bf16[128,8,2]{1,2,0:T(2,128)(2,1)} %copy.26), calls=%async_computation.1 | async-start | bytes 131072 | tf_op jit(solution)/shard_map/all_to_all | solution.py:105
  38.9 0.6 pad_add_fusion.6.ctl_ref
  39.5 7.4 %all-to-all-done.1 = bf16[128,8,2]{1,2,0:T(2,128)(2,1)S(1)} async-done(((bf16[128,8,2]{1,2,0:T(2,128)(2,1)}), bf16[128,8,2]{1,2,0:T(2,128)(2,1)S(1)}, u32[]{:S(2)}, u32[]{:S(2)}) %all-to-all-start.1) | async-done | bytes 4128 | tf_op jit(solution)/shard_map/all_to_all | solution.py:105
  47.1 9.6 %all-gather.2.cloned.1.call-done = bf16[2,512,512]{2,1,0:T(8,128)(2,1)} async-done(((bf16[2,512,128]{2,1,0:T(8,128)(2,1)}), bf16[2,512,512]{2,1,0:T(8,128)(2,1)}) %all-gather.2.cloned.1.call-update) | async-done | bytes 1048592 | tf_op jit(solution)/shard_map/all_gather | solution.py:112
  56.6 2.4 fusion.6
  59.1 0.8 fusion.12
  60.5 2.3 slice_bitcast_fusion
  62.7 8.3 %shard_map.37 = (bf16[4,512,512]{2,1,0:T(8,128)(2,1)}, bf16[4,128,512]{2,1,0:T(8,128)(2,1)}) custom-call(s32[2]{0:T(128)} %pad_add_fusion.6.ctl_ref, bf16[4,512,512]{2,1,0:T(8,128)(2,1)} %get-tuple-element.32.upper_ref, bf16[4,512,512]{2,1,0:T(8,128)(2,1)} %get-tuple-element.31.lower_ref), custom_call_target="tpu_custom_call" | custom-call | tf_op jit(solution)/shard_map/pallas_call | solution.py:84
  71.0 1.9 collective-permute-start
  72.9 10.9 %collective-permute-done = bf16[4,128,512]{2,1,0:T(8,128)(2,1)S(1)} collective-permute-done((bf16[4,128,512]{2,1,0:T(8,128)(2,1)}, bf16[4,128,512]{2,1,0:T(8,128)(2,1)S(1)}, u32[]{:S(2)}, u32[]{:S(2)}) %collective-permute-start) | collective-permute-done | bytes 524320 | tf_op jit(solution)/shard_map/ppermute | solution.py:17
  83.8 0.8 collective-permute-start.1
  84.6 2.7 collective-permute-start.2
  87.3 1.8 collective-permute-start.3
  89.8 9.8 %collective-permute-done.1 = bf16[4,128,512]{2,1,0:T(8,128)(2,1)S(1)} collective-permute-done((bf16[4,128,512]{2,1,0:T(8,128)(2,1)S(1)}, bf16[4,128,512]{2,1,0:T(8,128)(2,1)S(1)}, u32[]{:S(2)}, u32[]{:S(2)}) %collective-permute-start.1) | collective-permute-done | bytes 524320 | tf_op jit(solution)/shard_map/ppermute | solution.py:22
  99.6 8.0 %collective-permute-done.2 = bf16[4,128,512]{2,1,0:T(8,128)(2,1)S(1)} collective-permute-done((bf16[4,128,512]{2,1,0:T(8,128)(2,1)S(1)}, bf16[4,128,512]{2,1,0:T(8,128)(2,1)S(1)}, u32[]{:S(2)}, u32[]{:S(2)}) %collective-permute-start.2) | collective-permute-done | bytes 524320 | tf_op jit(solution)/shard_map/ppermute | solution.py:22
  107.9 1.6 pad_maximum_fusion.1.upper_ref
  109.5 8.4 %shard_map.38 = (bf16[4,512,512]{2,1,0:T(8,128)(2,1)}, bf16[4,128,512]{2,1,0:T(8,128)(2,1)}) custom-call(s32[2]{0:T(128)} %pad_add_fusion.5.ctl_ref, bf16[4,4,128,512]{3,2,1,0:T(8,128)(2,1)} %pad_maximum_fusion.1.upper_ref, bf16[4,512,512]{2,1,0:T(8,128)(2,1)} %get-tuple-element.19.lower_ref), custom_call_target="tpu_custom_call" | custom-call | tf_op jit(solution)/shard_map/pallas_call | solution.py:84
  118.0 3.5 collective-permute-start.4
  121.4 13.5 %collective-permute-done.4 = bf16[4,128,512]{2,1,0:T(8,128)(2,1)S(1)} collective-permute-done((bf16[4,128,512]{2,1,0:T(8,128)(2,1)}, bf16[4,128,512]{2,1,0:T(8,128)(2,1)S(1)}, u32[]{:S(2)}, u32[]{:S(2)}) %collective-permute-start.4) | collective-permute-done | bytes 524320 | tf_op jit(solution)/shard_map/ppermute | solution.py:17
  134.9 2.3 collective-permute-start.5
  137.3 2.8 collective-permute-start.6
  140.1 0.6 pad_add_fusion.4.ctl_ref
  140.7 9.9 %collective-permute-done.5 = bf16[4,128,512]{2,1,0:T(8,128)(2,1)S(1)} collective-permute-done((bf16[4,128,512]{2,1,0:T(8,128)(2,1)S(1)}, bf16[4,128,512]{2,1,0:T(8,128)(2,1)S(1)}, u32[]{:S(2)}, u32[]{:S(2)}) %collective-permute-start.5) | collective-permute-done | bytes 524320 | tf_op jit(solution)/shard_map/ppermute | solution.py:22
  150.6 11.7 %collective-permute-done.6 = bf16[4,128,512]{2,1,0:T(8,128)(2,1)S(1)} collective-permute-done((bf16[4,128,512]{2,1,0:T(8,128)(2,1)S(1)}, bf16[4,128,512]{2,1,0:T(8,128)(2,1)S(1)}, u32[]{:S(2)}, u32[]{:S(2)}) %collective-permute-start.6) | collective-permute-done | bytes 524320 | tf_op jit(solution)/shard_map/ppermute | solution.py:22
  162.3 1.6 pad_maximum_fusion.2.upper_ref
  163.9 8.3 %shard_map.39 = (bf16[4,512,512]{2,1,0:T(8,128)(2,1)}, bf16[4,128,512]{2,1,0:T(8,128)(2,1)}) custom-call(s32[2]{0:T(128)} %pad_add_fusion.4.ctl_ref, bf16[4,4,128,512]{3,2,1,0:T(8,128)(2,1)} %pad_maximum_fusion.2.upper_ref, bf16[4,512,512]{2,1,0:T(8,128)(2,1)} %get-tuple-element.21.lower_ref), custom_call_target="tpu_custom_call" | custom-call | tf_op jit(solution)/shard_map/pallas_call | solution.py:84
  172.2 2.7 collective-permute-start.8
  174.9 24.4 %collective-permute-done.8 = bf16[4,128,512]{2,1,0:T(8,128)(2,1)S(1)} collective-permute-done((bf16[4,128,512]{2,1,0:T(8,128)(2,1)}, bf16[4,128,512]{2,1,0:T(8,128)(2,1)S(1)}, u32[]{:S(2)}, u32[]{:S(2)}) %collective-permute-start.8) | collective-permute-done | bytes 524320 | tf_op jit(solution)/shard_map/ppermute | solution.py:17
  199.4 1.8 collective-permute-start.9
  201.2 3.3 collective-permute-start.10
  204.5 0.6 pad_add_fusion.3.ctl_ref
  205.1 9.9 %collective-permute-done.9 = bf16[4,128,512]{2,1,0:T(8,128)(2,1)S(1)} collective-permute-done((bf16[4,128,512]{2,1,0:T(8,128)(2,1)S(1)}, bf16[4,128,512]{2,1,0:T(8,128)(2,1)S(1)}, u32[]{:S(2)}, u32[]{:S(2)}) %collective-permute-start.9) | collective-permute-done | bytes 524320 | tf_op jit(solution)/shard_map/ppermute | solution.py:22
  215.0 12.0 %collective-permute-done.10 = bf16[4,128,512]{2,1,0:T(8,128)(2,1)S(1)} collective-permute-done((bf16[4,128,512]{2,1,0:T(8,128)(2,1)S(1)}, bf16[4,128,512]{2,1,0:T(8,128)(2,1)S(1)}, u32[]{:S(2)}, u32[]{:S(2)}) %collective-permute-start.10) | collective-permute-done | bytes 524320 | tf_op jit(solution)/shard_map/ppermute | solution.py:22
  227.0 1.6 pad_maximum_fusion.3.upper_ref
  228.6 8.5 %shard_map.40 = (bf16[4,512,512]{2,1,0:T(8,128)(2,1)}, bf16[4,128,512]{2,1,0:T(8,128)(2,1)}) custom-call(s32[2]{0:T(128)} %pad_add_fusion.3.ctl_ref, bf16[4,4,128,512]{3,2,1,0:T(8,128)(2,1)} %pad_maximum_fusion.3.upper_ref, bf16[4,512,512]{2,1,0:T(8,128)(2,1)} %get-tuple-element.23.lower_ref), custom_call_target="tpu_custom_call" | custom-call | tf_op jit(solution)/shard_map/pallas_call | solution.py:84
  237.1 6.8 %collective-permute-start.12 = (bf16[4,128,512]{2,1,0:T(8,128)(2,1)}, bf16[4,128,512]{2,1,0:T(8,128)(2,1)S(1)}, u32[]{:S(2)}, u32[]{:S(2)}) collective-permute-start(bf16[4,128,512]{2,1,0:T(8,128)(2,1)} %get-tuple-element.24), channel_id=1, source_target_pairs={{0,32},{4,36},{8,40},{12,44},{16,48},{20,52},{24,56},{28,60},{32,6... | collective-permute-start | bytes 1572872 | tf_op jit(solution)/shard_map/ppermute | solution.py:17
  243.9 23.5 %collective-permute-done.12 = bf16[4,128,512]{2,1,0:T(8,128)(2,1)S(1)} collective-permute-done((bf16[4,128,512]{2,1,0:T(8,128)(2,1)}, bf16[4,128,512]{2,1,0:T(8,128)(2,1)S(1)}, u32[]{:S(2)}, u32[]{:S(2)}) %collective-permute-start.12) | collective-permute-done | bytes 524320 | tf_op jit(solution)/shard_map/ppermute | solution.py:17
  267.4 1.6 collective-permute-start.13
  269.0 3.3 collective-permute-start.14
  272.3 0.6 pad_add_fusion.2.ctl_ref
  272.9 10.0 %collective-permute-done.13 = bf16[4,128,512]{2,1,0:T(8,128)(2,1)S(1)} collective-permute-done((bf16[4,128,512]{2,1,0:T(8,128)(2,1)S(1)}, bf16[4,128,512]{2,1,0:T(8,128)(2,1)S(1)}, u32[]{:S(2)}, u32[]{:S(2)}) %collective-permute-start.13) | collective-permute-done | bytes 524320 | tf_op jit(solution)/shard_map/ppermute | solution.py:22
  282.9 12.4 %collective-permute-done.14 = bf16[4,128,512]{2,1,0:T(8,128)(2,1)S(1)} collective-permute-done((bf16[4,128,512]{2,1,0:T(8,128)(2,1)S(1)}, bf16[4,128,512]{2,1,0:T(8,128)(2,1)S(1)}, u32[]{:S(2)}, u32[]{:S(2)}) %collective-permute-start.14) | collective-permute-done | bytes 524320 | tf_op jit(solution)/shard_map/ppermute | solution.py:22
  295.4 1.6 pad_maximum_fusion.4.upper_ref
  297.0 8.3 %shard_map.41 = (bf16[4,512,512]{2,1,0:T(8,128)(2,1)}, bf16[4,128,512]{2,1,0:T(8,128)(2,1)}) custom-call(s32[2]{0:T(128)} %pad_add_fusion.2.ctl_ref, bf16[4,4,128,512]{3,2,1,0:T(8,128)(2,1)} %pad_maximum_fusion.4.upper_ref, bf16[4,512,512]{2,1,0:T(8,128)(2,1)} %get-tuple-element.25.lower_ref), custom_call_target="tpu_custom_call" | custom-call | tf_op jit(solution)/shard_map/pallas_call | solution.py:84
  305.2 2.0 collective-permute-start.16
  307.2 13.1 %collective-permute-done.16 = bf16[4,128,512]{2,1,0:T(8,128)(2,1)S(1)} collective-permute-done((bf16[4,128,512]{2,1,0:T(8,128)(2,1)}, bf16[4,128,512]{2,1,0:T(8,128)(2,1)S(1)}, u32[]{:S(2)}, u32[]{:S(2)}) %collective-permute-start.16) | collective-permute-done | bytes 524320 | tf_op jit(solution)/shard_map/ppermute | solution.py:17
  320.3 1.1 collective-permute-start.17
  321.4 3.3 collective-permute-start.18
  325.3 9.9 %collective-permute-done.17 = bf16[4,128,512]{2,1,0:T(8,128)(2,1)S(1)} collective-permute-done((bf16[4,128,512]{2,1,0:T(8,128)(2,1)S(1)}, bf16[4,128,512]{2,1,0:T(8,128)(2,1)S(1)}, u32[]{:S(2)}, u32[]{:S(2)}) %collective-permute-start.17) | collective-permute-done | bytes 524320 | tf_op jit(solution)/shard_map/ppermute | solution.py:22
  335.2 11.7 %collective-permute-done.18 = bf16[4,128,512]{2,1,0:T(8,128)(2,1)S(1)} collective-permute-done((bf16[4,128,512]{2,1,0:T(8,128)(2,1)S(1)}, bf16[4,128,512]{2,1,0:T(8,128)(2,1)S(1)}, u32[]{:S(2)}, u32[]{:S(2)}) %collective-permute-start.18) | collective-permute-done | bytes 524320 | tf_op jit(solution)/shard_map/ppermute | solution.py:22
  346.9 1.6 pad_maximum_fusion.5.upper_ref
  348.5 8.5 %shard_map.42 = (bf16[4,512,512]{2,1,0:T(8,128)(2,1)}, bf16[4,128,512]{2,1,0:T(8,128)(2,1)}) custom-call(s32[2]{0:T(128)} %pad_add_fusion.1.ctl_ref, bf16[4,4,128,512]{3,2,1,0:T(8,128)(2,1)} %pad_maximum_fusion.5.upper_ref, bf16[4,512,512]{2,1,0:T(8,128)(2,1)} %get-tuple-element.27.lower_ref), custom_call_target="tpu_custom_call" | custom-call | tf_op jit(solution)/shard_map/pallas_call | solution.py:84
  357.0 1.3 collective-permute-start.20
  358.3 14.5 %collective-permute-done.20 = bf16[4,128,512]{2,1,0:T(8,128)(2,1)S(1)} collective-permute-done((bf16[4,128,512]{2,1,0:T(8,128)(2,1)}, bf16[4,128,512]{2,1,0:T(8,128)(2,1)S(1)}, u32[]{:S(2)}, u32[]{:S(2)}) %collective-permute-start.20) | collective-permute-done | bytes 524320 | tf_op jit(solution)/shard_map/ppermute | solution.py:17
  372.9 1.9 collective-permute-start.21
  374.7 3.3 collective-permute-start.22
  378.6 9.9 %collective-permute-done.21 = bf16[4,128,512]{2,1,0:T(8,128)(2,1)S(1)} collective-permute-done((bf16[4,128,512]{2,1,0:T(8,128)(2,1)S(1)}, bf16[4,128,512]{2,1,0:T(8,128)(2,1)S(1)}, u32[]{:S(2)}, u32[]{:S(2)}) %collective-permute-start.21) | collective-permute-done | bytes 524320 | tf_op jit(solution)/shard_map/ppermute | solution.py:22
  388.5 11.7 %collective-permute-done.22 = bf16[4,128,512]{2,1,0:T(8,128)(2,1)S(1)} collective-permute-done((bf16[4,128,512]{2,1,0:T(8,128)(2,1)S(1)}, bf16[4,128,512]{2,1,0:T(8,128)(2,1)S(1)}, u32[]{:S(2)}, u32[]{:S(2)}) %collective-permute-start.22) | collective-permute-done | bytes 524320 | tf_op jit(solution)/shard_map/ppermute | solution.py:22
  400.2 1.6 pad_maximum_fusion.6.upper_ref
  401.8 8.3 %shard_map.43 = (bf16[4,512,512]{2,1,0:T(8,128)(2,1)}, bf16[4,128,512]{2,1,0:T(8,128)(2,1)}) custom-call(s32[2]{0:T(128)} %pad_add_fusion.ctl_ref, bf16[4,4,128,512]{3,2,1,0:T(8,128)(2,1)} %pad_maximum_fusion.6.upper_ref, bf16[4,512,512]{2,1,0:T(8,128)(2,1)} %get-tuple-element.29.lower_ref), custom_call_target="tpu_custom_call" | custom-call | tf_op jit(solution)/shard_map/pallas_call | solution.py:84
  (27 shorter events, 3.0 us)
Async XLA Ops:
  6.5 50.1 %all-gather.2.cloned.1.call-start = ((), (), s32[]{:S(2)}) async-start(), calls=%async_computation.2 | async-start | bytes 1310720 | tf_op jit(solution)/shard_map/all_gather | solution.py:112
  32.4 14.5 %all-to-all-start.1 = ((bf16[128,8,2]{1,2,0:T(2,128)(2,1)}), bf16[128,8,2]{1,2,0:T(2,128)(2,1)S(1)}, u32[]{:S(2)}, u32[]{:S(2)}) async-start(bf16[128,8,2]{1,2,0:T(2,128)(2,1)} %copy.26), calls=%async_computation.1 | async-start | bytes 131072 | tf_op jit(solution)/shard_map/all_to_all | solution.py:105
  56.6 2.5 copy-start
  71.0 12.8 %collective-permute-start = (bf16[4,128,512]{2,1,0:T(8,128)(2,1)}, bf16[4,128,512]{2,1,0:T(8,128)(2,1)S(1)}, u32[]{:S(2)}, u32[]{:S(2)}) collective-permute-start(bf16[4,128,512]{2,1,0:T(8,128)(2,1)} %get-tuple-element.18), channel_id=1, source_target_pairs={{0,4},{4,8},{8,12},{12,16},{16,20},{20,24},{24,28},{28,32},{32,36}... | collective-permute-start | bytes 1572872 | tf_op jit(solution)/shard_map/ppermute | solution.py:17
  83.8 15.8 %collective-permute-start.1 = (bf16[4,128,512]{2,1,0:T(8,128)(2,1)S(1)}, bf16[4,128,512]{2,1,0:T(8,128)(2,1)S(1)}, u32[]{:S(2)}, u32[]{:S(2)}) collective-permute-start(bf16[4,128,512]{2,1,0:T(8,128)(2,1)S(1)} %collective-permute-done), channel_id=1, source_target_pairs={{0,1},{1,2},{2,3},{3,0},{4,5},{5,6},{6,7},{7,4},{8,9},{9,10},{10,1... | collective-permute-start | bytes 1572872 | tf_op jit(solution)/shard_map/ppermute | solution.py:22
  84.6 22.9 %collective-permute-start.2 = (bf16[4,128,512]{2,1,0:T(8,128)(2,1)S(1)}, bf16[4,128,512]{2,1,0:T(8,128)(2,1)S(1)}, u32[]{:S(2)}, u32[]{:S(2)}) collective-permute-start(bf16[4,128,512]{2,1,0:T(8,128)(2,1)S(1)} %collective-permute-done), channel_id=1, source_target_pairs={{0,2},{1,3},{2,0},{3,1},{4,6},{5,7},{6,4},{7,5},{8,10},{9,11},{10,... | collective-permute-start | bytes 1572872 | tf_op jit(solution)/shard_map/ppermute | solution.py:22
  87.3 20.6 %collective-permute-start.3 = (bf16[4,128,512]{2,1,0:T(8,128)(2,1)S(1)}, bf16[4,128,512]{2,1,0:T(8,128)(2,1)S(1)}, u32[]{:S(2)}, u32[]{:S(2)}) collective-permute-start(bf16[4,128,512]{2,1,0:T(8,128)(2,1)S(1)} %collective-permute-done), channel_id=1, source_target_pairs={{0,3},{1,0},{2,1},{3,2},{4,7},{5,4},{6,5},{7,6},{8,11},{9,8},{10,9... | collective-permute-start | bytes 1572872 | tf_op jit(solution)/shard_map/ppermute | solution.py:22
  118.0 17.0 %collective-permute-start.4 = (bf16[4,128,512]{2,1,0:T(8,128)(2,1)}, bf16[4,128,512]{2,1,0:T(8,128)(2,1)S(1)}, u32[]{:S(2)}, u32[]{:S(2)}) collective-permute-start(bf16[4,128,512]{2,1,0:T(8,128)(2,1)} %get-tuple-element.20), channel_id=1, source_target_pairs={{0,8},{4,12},{8,16},{12,20},{16,24},{20,28},{24,32},{28,36},{32,40... | collective-permute-start | bytes 1572872 | tf_op jit(solution)/shard_map/ppermute | solution.py:17
  134.9 15.6 %collective-permute-start.5 = (bf16[4,128,512]{2,1,0:T(8,128)(2,1)S(1)}, bf16[4,128,512]{2,1,0:T(8,128)(2,1)S(1)}, u32[]{:S(2)}, u32[]{:S(2)}) collective-permute-start(bf16[4,128,512]{2,1,0:T(8,128)(2,1)S(1)} %collective-permute-done.4), channel_id=1, source_target_pairs={{0,1},{1,2},{2,3},{3,0},{4,5},{5,6},{6,7},{7,4},{8,9},{9,10},{10,1... | collective-permute-start | bytes 1572872 | tf_op jit(solution)/shard_map/ppermute | solution.py:22
  137.3 25.0 %collective-permute-start.6 = (bf16[4,128,512]{2,1,0:T(8,128)(2,1)S(1)}, bf16[4,128,512]{2,1,0:T(8,128)(2,1)S(1)}, u32[]{:S(2)}, u32[]{:S(2)}) collective-permute-start(bf16[4,128,512]{2,1,0:T(8,128)(2,1)S(1)} %collective-permute-done.4), channel_id=1, source_target_pairs={{0,2},{1,3},{2,0},{3,1},{4,6},{5,7},{6,4},{7,5},{8,10},{9,11},{10,... | collective-permute-start | bytes 1572872 | tf_op jit(solution)/shard_map/ppermute | solution.py:22
  140.1 22.2 %collective-permute-start.7 = (bf16[4,128,512]{2,1,0:T(8,128)(2,1)S(1)}, bf16[4,128,512]{2,1,0:T(8,128)(2,1)S(1)}, u32[]{:S(2)}, u32[]{:S(2)}) collective-permute-start(bf16[4,128,512]{2,1,0:T(8,128)(2,1)S(1)} %collective-permute-done.4), channel_id=1, source_target_pairs={{0,3},{1,0},{2,1},{3,2},{4,7},{5,4},{6,5},{7,6},{8,11},{9,8},{10,9... | collective-permute-start | bytes 1572872 | tf_op jit(solution)/shard_map/ppermute | solution.py:22
  172.2 27.2 %collective-permute-start.8 = (bf16[4,128,512]{2,1,0:T(8,128)(2,1)}, bf16[4,128,512]{2,1,0:T(8,128)(2,1)S(1)}, u32[]{:S(2)}, u32[]{:S(2)}) collective-permute-start(bf16[4,128,512]{2,1,0:T(8,128)(2,1)} %get-tuple-element.22), channel_id=1, source_target_pairs={{0,16},{4,20},{8,24},{12,28},{16,32},{20,36},{24,40},{28,44},{32,4... | collective-permute-start | bytes 1572872 | tf_op jit(solution)/shard_map/ppermute | solution.py:17
  199.4 15.6 %collective-permute-start.9 = (bf16[4,128,512]{2,1,0:T(8,128)(2,1)S(1)}, bf16[4,128,512]{2,1,0:T(8,128)(2,1)S(1)}, u32[]{:S(2)}, u32[]{:S(2)}) collective-permute-start(bf16[4,128,512]{2,1,0:T(8,128)(2,1)S(1)} %collective-permute-done.8), channel_id=1, source_target_pairs={{0,1},{1,2},{2,3},{3,0},{4,5},{5,6},{6,7},{7,4},{8,9},{9,10},{10,1... | collective-permute-start | bytes 1572872 | tf_op jit(solution)/shard_map/ppermute | solution.py:22
  201.2 25.8 %collective-permute-start.10 = (bf16[4,128,512]{2,1,0:T(8,128)(2,1)S(1)}, bf16[4,128,512]{2,1,0:T(8,128)(2,1)S(1)}, u32[]{:S(2)}, u32[]{:S(2)}) collective-permute-start(bf16[4,128,512]{2,1,0:T(8,128)(2,1)S(1)} %collective-permute-done.8), channel_id=1, source_target_pairs={{0,2},{1,3},{2,0},{3,1},{4,6},{5,7},{6,4},{7,5},{8,10},{9,11},{10,... | collective-permute-start | bytes 1572872 | tf_op jit(solution)/shard_map/ppermute | solution.py:22
  204.5 22.4 %collective-permute-start.11 = (bf16[4,128,512]{2,1,0:T(8,128)(2,1)S(1)}, bf16[4,128,512]{2,1,0:T(8,128)(2,1)S(1)}, u32[]{:S(2)}, u32[]{:S(2)}) collective-permute-start(bf16[4,128,512]{2,1,0:T(8,128)(2,1)S(1)} %collective-permute-done.8), channel_id=1, source_target_pairs={{0,3},{1,0},{2,1},{3,2},{4,7},{5,4},{6,5},{7,6},{8,11},{9,8},{10,9... | collective-permute-start | bytes 1572872 | tf_op jit(solution)/shard_map/ppermute | solution.py:22
  237.1 30.3 %collective-permute-start.12 = (bf16[4,128,512]{2,1,0:T(8,128)(2,1)}, bf16[4,128,512]{2,1,0:T(8,128)(2,1)S(1)}, u32[]{:S(2)}, u32[]{:S(2)}) collective-permute-start(bf16[4,128,512]{2,1,0:T(8,128)(2,1)} %get-tuple-element.24), channel_id=1, source_target_pairs={{0,32},{4,36},{8,40},{12,44},{16,48},{20,52},{24,56},{28,60},{32,6... | collective-permute-start | bytes 1572872 | tf_op jit(solution)/shard_map/ppermute | solution.py:17
  267.4 15.6 %collective-permute-start.13 = (bf16[4,128,512]{2,1,0:T(8,128)(2,1)S(1)}, bf16[4,128,512]{2,1,0:T(8,128)(2,1)S(1)}, u32[]{:S(2)}, u32[]{:S(2)}) collective-permute-start(bf16[4,128,512]{2,1,0:T(8,128)(2,1)S(1)} %collective-permute-done.12), channel_id=1, source_target_pairs={{0,1},{1,2},{2,3},{3,0},{4,5},{5,6},{6,7},{7,4},{8,9},{9,10},{10,1... | collective-permute-start | bytes 1572872 | tf_op jit(solution)/shard_map/ppermute | solution.py:22
  269.0 26.4 %collective-permute-start.14 = (bf16[4,128,512]{2,1,0:T(8,128)(2,1)S(1)}, bf16[4,128,512]{2,1,0:T(8,128)(2,1)S(1)}, u32[]{:S(2)}, u32[]{:S(2)}) collective-permute-start(bf16[4,128,512]{2,1,0:T(8,128)(2,1)S(1)} %collective-permute-done.12), channel_id=1, source_target_pairs={{0,2},{1,3},{2,0},{3,1},{4,6},{5,7},{6,4},{7,5},{8,10},{9,11},{10,... | collective-permute-start | bytes 1572872 | tf_op jit(solution)/shard_map/ppermute | solution.py:22
  272.3 23.1 %collective-permute-start.15 = (bf16[4,128,512]{2,1,0:T(8,128)(2,1)S(1)}, bf16[4,128,512]{2,1,0:T(8,128)(2,1)S(1)}, u32[]{:S(2)}, u32[]{:S(2)}) collective-permute-start(bf16[4,128,512]{2,1,0:T(8,128)(2,1)S(1)} %collective-permute-done.12), channel_id=1, source_target_pairs={{0,3},{1,0},{2,1},{3,2},{4,7},{5,4},{6,5},{7,6},{8,11},{9,8},{10,9... | collective-permute-start | bytes 1572872 | tf_op jit(solution)/shard_map/ppermute | solution.py:22
  305.2 15.1 %collective-permute-start.16 = (bf16[4,128,512]{2,1,0:T(8,128)(2,1)}, bf16[4,128,512]{2,1,0:T(8,128)(2,1)S(1)}, u32[]{:S(2)}, u32[]{:S(2)}) collective-permute-start(bf16[4,128,512]{2,1,0:T(8,128)(2,1)} %get-tuple-element.26), channel_id=1, source_target_pairs={{0,64},{4,68},{8,72},{12,76},{16,80},{20,84},{24,88},{28,92},{32,9... | collective-permute-start | bytes 1572872 | tf_op jit(solution)/shard_map/ppermute | solution.py:17
  320.3 14.8 %collective-permute-start.17 = (bf16[4,128,512]{2,1,0:T(8,128)(2,1)S(1)}, bf16[4,128,512]{2,1,0:T(8,128)(2,1)S(1)}, u32[]{:S(2)}, u32[]{:S(2)}) collective-permute-start(bf16[4,128,512]{2,1,0:T(8,128)(2,1)S(1)} %collective-permute-done.16), channel_id=1, source_target_pairs={{0,1},{1,2},{2,3},{3,0},{4,5},{5,6},{6,7},{7,4},{8,9},{9,10},{10,1... | collective-permute-start | bytes 1572872 | tf_op jit(solution)/shard_map/ppermute | solution.py:22
  321.4 25.5 %collective-permute-start.18 = (bf16[4,128,512]{2,1,0:T(8,128)(2,1)S(1)}, bf16[4,128,512]{2,1,0:T(8,128)(2,1)S(1)}, u32[]{:S(2)}, u32[]{:S(2)}) collective-permute-start(bf16[4,128,512]{2,1,0:T(8,128)(2,1)S(1)} %collective-permute-done.16), channel_id=1, source_target_pairs={{0,2},{1,3},{2,0},{3,1},{4,6},{5,7},{6,4},{7,5},{8,10},{9,11},{10,... | collective-permute-start | bytes 1572872 | tf_op jit(solution)/shard_map/ppermute | solution.py:22
  324.7 22.2 %collective-permute-start.19 = (bf16[4,128,512]{2,1,0:T(8,128)(2,1)S(1)}, bf16[4,128,512]{2,1,0:T(8,128)(2,1)S(1)}, u32[]{:S(2)}, u32[]{:S(2)}) collective-permute-start(bf16[4,128,512]{2,1,0:T(8,128)(2,1)S(1)} %collective-permute-done.16), channel_id=1, source_target_pairs={{0,3},{1,0},{2,1},{3,2},{4,7},{5,4},{6,5},{7,6},{8,11},{9,8},{10,9... | collective-permute-start | bytes 1572872 | tf_op jit(solution)/shard_map/ppermute | solution.py:22
  357.0 15.8 %collective-permute-start.20 = (bf16[4,128,512]{2,1,0:T(8,128)(2,1)}, bf16[4,128,512]{2,1,0:T(8,128)(2,1)S(1)}, u32[]{:S(2)}, u32[]{:S(2)}) collective-permute-start(bf16[4,128,512]{2,1,0:T(8,128)(2,1)} %get-tuple-element.28), channel_id=1, source_target_pairs={{0,128},{4,132},{8,136},{12,140},{16,144},{20,148},{24,152},{28,15... | collective-permute-start | bytes 1572872 | tf_op jit(solution)/shard_map/ppermute | solution.py:17
  372.9 15.6 %collective-permute-start.21 = (bf16[4,128,512]{2,1,0:T(8,128)(2,1)S(1)}, bf16[4,128,512]{2,1,0:T(8,128)(2,1)S(1)}, u32[]{:S(2)}, u32[]{:S(2)}) collective-permute-start(bf16[4,128,512]{2,1,0:T(8,128)(2,1)S(1)} %collective-permute-done.20), channel_id=1, source_target_pairs={{0,1},{1,2},{2,3},{3,0},{4,5},{5,6},{6,7},{7,4},{8,9},{9,10},{10,1... | collective-permute-start | bytes 1572872 | tf_op jit(solution)/shard_map/ppermute | solution.py:22
  374.7 25.5 %collective-permute-start.22 = (bf16[4,128,512]{2,1,0:T(8,128)(2,1)S(1)}, bf16[4,128,512]{2,1,0:T(8,128)(2,1)S(1)}, u32[]{:S(2)}, u32[]{:S(2)}) collective-permute-start(bf16[4,128,512]{2,1,0:T(8,128)(2,1)S(1)} %collective-permute-done.20), channel_id=1, source_target_pairs={{0,2},{1,3},{2,0},{3,1},{4,6},{5,7},{6,4},{7,5},{8,10},{9,11},{10,... | collective-permute-start | bytes 1572872 | tf_op jit(solution)/shard_map/ppermute | solution.py:22
  378.0 22.2 %collective-permute-start.23 = (bf16[4,128,512]{2,1,0:T(8,128)(2,1)S(1)}, bf16[4,128,512]{2,1,0:T(8,128)(2,1)S(1)}, u32[]{:S(2)}, u32[]{:S(2)}) collective-permute-start(bf16[4,128,512]{2,1,0:T(8,128)(2,1)S(1)} %collective-permute-done.20), channel_id=1, source_target_pairs={{0,3},{1,0},{2,1},{3,2},{4,7},{5,4},{6,5},{7,6},{8,11},{9,8},{10,9... | collective-permute-start | bytes 1572872 | tf_op jit(solution)/shard_map/ppermute | solution.py:22
Sparse Core Ops, SparseCore 0:
  31.0 25.5 all-gather.1
